TPU v7x, 256 devices: a whole 4x4x8 slice. The times are simulated.
256 devices in a mesh: row: 8 (over z_hi, y), col: 32 (over x, z_lo, core).
Axes of the slice: x: 4, y: 4, z: 8 (z_hi: 2, z_lo: 4; z = z_hi * 4 + z_lo), core: 2. Of those that a mesh axis runs over, the one named last changes fastest.
Arguments:
- features: bfloat16 [65536, 256], P(('row', 'col')), may hold values from -6 to 6
- weight: bfloat16 [256, 256], replicated, may hold values from -0.375 to 0.375
- cotangent: bfloat16 [65536, 256], P(('row', 'col')), may hold values from -6 to 6
- tile_values: bfloat16 [8, 8192, 128, 128], P('row', 'col'), may hold values from -0.0625 to 0.0625
- tile_rows: int32 [8, 8192], P('row', 'col'), may hold values from 0 to 63, as said below
- tile_cols: int32 [8, 8192], P('row', 'col'), may hold values from 0 to 15
- tile_count: int32 [8, 32], P('row', 'col'), may hold values from 32 to 256
Outputs:
- output: bfloat16 [65536, 256], P(('row', 'col'))
- feature_grad: bfloat16 [65536, 256], P(('row', 'col'))
- weight_grad: float32 [256, 256], replicated
Inputs may be any that keep to these rules, and one draw needn't show every extreme that they name: Within one grid block's 256 entries the pairs (tile_rows, tile_cols) are distinct; only the first tile_count entries are occupied tiles.
All inputs are finite; a program needn't handle non-finite values.
Results may differ from a plain program's by a relative error of at most 0.006.
Values may be sent and summed in bfloat16 or wider, within the bound.
No kernel may reach another device: no remote copies, remote signals or barrier semaphores. Data moves between devices by JAX's collectives and lax.ppermute only.
A program may use at most 128 MiB of HBM per device.

v0:
```python
import jax
import jax.numpy as jnp
from jax import lax
from jax.experimental import pallas as pl
from jax.experimental.pallas import tpu as pltpu
from jax.sharding import Mesh
from jax.sharding import PartitionSpec as P

GROUP = 64


def tile_product(
    tile_block, row_ids, col_ids, occupied, source, out_rows, transpose, out_dtype,
    cores=1, dev_tiles=1,
):
    tile_count, tile_side, _ = tile_block.shape
    feat_width = source.shape[1]
    src_rows = source.shape[0]
    row_limit = (src_rows if transpose else out_rows) // tile_side - 1
    col_limit = (out_rows if transpose else src_rows) // tile_side - 1
    steps = tile_count // GROUP
    out_tiles = out_rows // tile_side

    def kernel(rows_ref, cols_ref, cnt_ref, tiles_ref, src_ref, out_ref, acc_ref):
        g = pl.program_id(0)
        cnt = cnt_ref[0]

        @pl.when(g == 0)
        def _():
            acc_ref[...] = jnp.zeros_like(acc_ref)

        @pl.when(g * GROUP < cnt)
        def _():
            for t in range(GROUP):
                k = g * GROUP + t
                r = jnp.clip(rows_ref[k], 0, row_limit)
                c = jnp.clip(cols_ref[k], 0, col_limit)
                a = tiles_ref[t]
                if transpose:
                    s = src_ref[pl.ds(pl.multiple_of(r * tile_side, tile_side), tile_side), :]
                    prod = lax.dot_general(
                        a, s, (((0,), (0,)), ((), ())), preferred_element_type=jnp.float32
                    )
                    dst = c
                else:
                    s = src_ref[pl.ds(pl.multiple_of(c * tile_side, tile_side), tile_side), :]
                    prod = jnp.dot(a, s, preferred_element_type=jnp.float32)
                    dev, part = r // dev_tiles, r % dev_tiles
                    per_core = out_tiles // dev_tiles // cores
                    dst = ((dev % cores) * per_core + dev // cores) * dev_tiles + part
                prod = jnp.where(k < cnt, prod, 0.0)
                sl = pl.ds(pl.multiple_of(dst * tile_side, tile_side), tile_side)
                acc_ref[sl, :] += prod

        @pl.when(g == steps - 1)
        def _():
            out_ref[...] = acc_ref[...].astype(out_ref.dtype)

    def tile_map(g, rows_ref, cols_ref, cnt_ref):
        last = jnp.maximum(cnt_ref[0] - 1, 0) // GROUP
        return (jnp.minimum(g, last), 0, 0)

    grid_spec = pltpu.PrefetchScalarGridSpec(
        num_scalar_prefetch=3,
        grid=(steps,),
        in_specs=[
            pl.BlockSpec((GROUP, tile_side, tile_side), tile_map),
            pl.BlockSpec((src_rows, feat_width), lambda g, *_: (0, 0)),
        ],
        out_specs=pl.BlockSpec((out_rows, feat_width), lambda g, *_: (0, 0)),
        scratch_shapes=[pltpu.VMEM((out_rows, feat_width), jnp.float32)],
    )
    return pl.pallas_call(
        kernel,
        grid_spec=grid_spec,
        out_shape=jax.ShapeDtypeStruct((out_rows, feat_width), out_dtype),
        compiler_params=pltpu.CompilerParams(
            dimension_semantics=("arbitrary",), vmem_limit_bytes=48 * 1024 * 1024
        ),
    )(row_ids, col_ids, occupied.reshape(1), tile_block, source)


def reduce_blocks(partial_value, axis, devices):
    pieces = partial_value.reshape(devices, -1, partial_value.shape[1])
    received = lax.all_to_all(pieces, axis, 0, 0, tiled=False)
    return received.astype(jnp.float32).sum(0)


def butterfly_sum(value, axes):
    for axis in axes:
        size = lax.axis_size(axis)
        step = 1
        while step < size:
            pairs = [(i, i ^ step) for i in range(size)]
            value = value + lax.ppermute(value, axis, pairs)
            step *= 2
    return value


def split_sum(value, outer, inner):
    plan = []
    for axis in outer:
        step = 1
        while step < lax.axis_size(axis):
            plan.append((axis, step))
            step *= 2
    for axis, step in plan:
        size = lax.axis_size(axis)
        low = (lax.axis_index(axis) // step) % 2 == 0
        half = value.shape[0] // 2
        head, tail = value[:half], value[half:]
        send = jnp.where(low, tail, head)
        keep = jnp.where(low, head, tail)
        value = keep + lax.ppermute(send, axis, [(i, i ^ step) for i in range(size)])
    value = butterfly_sum(value, inner)
    for axis, step in reversed(plan):
        size = lax.axis_size(axis)
        low = (lax.axis_index(axis) // step) % 2 == 0
        other = lax.ppermute(value, axis, [(i, i ^ step) for i in range(size)])
        value = jnp.concatenate(
            [jnp.where(low, value, other), jnp.where(low, other, value)], axis=0
        )
    return value


def gather_pairs(value, axis):
    size = lax.axis_size(axis)
    me = lax.axis_index(axis)
    step = 1
    while step < size:
        other = lax.ppermute(value, axis, [(i, i ^ step) for i in range(size)])
        first = (me // step) % 2 == 0
        value = jnp.concatenate(
            [jnp.where(first, value, other), jnp.where(first, other, value)], axis=0
        )
        step *= 2
    return value


def reduce_pairs_then_blocks(partial_value, outer, inner):
    outer_size = lax.axis_size(outer)
    inner_size = lax.axis_size(inner)
    pieces = partial_value.reshape(inner_size, outer_size, -1, partial_value.shape[1])
    me = lax.axis_index(inner)
    keep = lax.dynamic_index_in_dim(pieces, me, 0, keepdims=False)
    send = lax.dynamic_index_in_dim(pieces, inner_size - 1 - me, 0, keepdims=False)
    paired = keep + lax.ppermute(send, inner, [(i, inner_size - 1 - i) for i in range(inner_size)])
    received = lax.all_to_all(paired.astype(jnp.bfloat16), outer, 0, 0, tiled=False)
    return received.astype(jnp.float32).sum(0)


def silu_grad(cot_part, pre_part):
    sigma = jax.nn.sigmoid(pre_part)
    return (cot_part.astype(jnp.float32) * (sigma * (1.0 + pre_part * (1.0 - sigma)))).astype(
        jnp.bfloat16
    )


def per_device(features, weight, cotangent, tile_values, tile_rows, tile_cols, tile_count):
    node_rows = features.shape[0]
    row_devices = lax.axis_size("row")
    col_axes = ("colhi", "core")
    col_devices = lax.axis_size(col_axes)
    tile_block = tile_values[0]
    row_ids = tile_rows[0]
    col_ids = tile_cols[0]
    occupied = tile_count[0, 0]
    column_source = gather_pairs(features, "row")
    partial_value = tile_product(
        tile_block, row_ids, col_ids, occupied, column_source, col_devices * node_rows, False,
        jnp.float32, cores=lax.axis_size("core"), dev_tiles=node_rows // tile_block.shape[1],
    )
    mixed = reduce_pairs_then_blocks(partial_value, "colhi", "core")
    pre = jnp.dot(
        mixed, weight.astype(jnp.float32), precision=lax.Precision.HIGHEST,
        preferred_element_type=jnp.float32,
    )
    grad_pre = silu_grad(cotangent, pre)
    local_term = lax.dot_general(
        mixed, grad_pre.astype(jnp.float32), (((0,), (0,)), ((), ())),
        precision=lax.Precision.HIGHEST, preferred_element_type=jnp.float32,
    )
    grad_scale = float(node_rows * row_devices * col_devices) ** (-0.5)
    weight_grad = split_sum(local_term, ("row",), ("core", "colhi")) * grad_scale
    row_source = lax.all_gather(grad_pre, col_axes, axis=0, tiled=True)
    row_source, weight_grad = lax.optimization_barrier((row_source, weight_grad))
    output = jax.nn.silu(pre).astype(jnp.bfloat16)
    back_terms = tile_product(
        tile_block, row_ids, col_ids, occupied, row_source, row_devices * node_rows, True,
        jnp.bfloat16,
    )
    aggregated = reduce_blocks(back_terms, "row", row_devices)
    node_grad = aggregated.astype(jnp.bfloat16)
    feature_grad = jnp.dot(node_grad, weight.T, preferred_element_type=jnp.float32).astype(
        jnp.bfloat16
    )
    return (output, feature_grad, weight_grad)


def solution(mesh):
    cores = 2
    devices = mesh.devices.reshape(mesh.shape["row"], mesh.shape["col"] // cores, cores)
    split_mesh = Mesh(devices, ("row", "colhi", "core"))
    nodes = ("row", "colhi", "core")
    blocks = ("colhi", "core")
    placed = (
        P(nodes, None),
        P(),
        P(nodes, None),
        P("row", blocks, None, None),
        P("row", blocks),
        P("row", blocks),
        P("row", blocks),
    )
    return jax.shard_map(
        per_device,
        mesh=split_mesh,
        in_specs=placed,
        out_specs=(P(nodes, None), P(nodes, None), P()),
        check_vma=False,
    )
```

profile of v0, /device:TPU:4, one launch (start us, length us, event | category | flops | bytes accessed | tf_op | source)
XLA Modules:
  0.0 250.8 jit_solution(16641305053221635838)
XLA Ops:
  7.2 0.0 all-gather.2.cloned.1.call-start
  7.2 1.7 collective-permute-start
  8.9 3.9 %collective-permute-done = bf16[256,256]{1,0:T(8,128)(2,1)S(1)} collective-permute-done((bf16[256,256]{1,0:T(8,128)(2,1)}, bf16[256,256]{1,0:T(8,128)(2,1)S(1)}, u32[]{:S(2)}, u32[]{:S(2)}) %collective-permute-start) | collective-permute-done | bytes 131104 | tf_op jit(solution)/shard_map/ppermute | solution.py:131
  12.8 0.9 broadcast_select_fusion.5
  13.7 3.3 %collective-permute-start.1 = (bf16[512,256]{1,0:T(8,128)(2,1)S(1)}, bf16[512,256]{1,0:T(8,128)(2,1)S(1)}, u32[]{:S(2)}, u32[]{:S(2)}) collective-permute-start(bf16[512,256]{1,0:T(8,128)(2,1)S(1)} %pad_maximum_fusion.2), channel_id=1, source_target_pairs={{0,64},{32,96},{64,0},{96,32},{128,192},{160,224},{192,128},{224,1... | collective-permute-start | bytes 786440 | tf_op jit(solution)/shard_map/ppermute | solution.py:131
  17.0 5.5 %collective-permute-done.1 = bf16[512,256]{1,0:T(8,128)(2,1)S(1)} collective-permute-done((bf16[512,256]{1,0:T(8,128)(2,1)S(1)}, bf16[512,256]{1,0:T(8,128)(2,1)S(1)}, u32[]{:S(2)}, u32[]{:S(2)}) %collective-permute-start.1) | collective-permute-done | bytes 262176 | tf_op jit(solution)/shard_map/ppermute | solution.py:131
  22.5 0.1 broadcast_select_fusion.3
  22.7 7.3 %collective-permute-start.2 = (bf16[1024,256]{1,0:T(8,128)(2,1)S(1)}, bf16[1024,256]{1,0:T(8,128)(2,1)S(1)}, u32[]{:S(2)}, u32[]{:S(2)}) collective-permute-start(bf16[1024,256]{1,0:T(8,128)(2,1)S(1)} %pad_maximum_fusion.1), channel_id=1, source_target_pairs={{0,128},{32,160},{64,192},{96,224},{128,0},{160,32},{192,64},{224,... | collective-permute-start | bytes 1572872 | tf_op jit(solution)/shard_map/ppermute | solution.py:131
  30.6 11.8 %collective-permute-done.2 = bf16[1024,256]{1,0:T(8,128)(2,1)S(1)} collective-permute-done((bf16[1024,256]{1,0:T(8,128)(2,1)S(1)}, bf16[1024,256]{1,0:T(8,128)(2,1)S(1)}, u32[]{:S(2)}, u32[]{:S(2)}) %collective-permute-start.2) | collective-permute-done | bytes 524320 | tf_op jit(solution)/shard_map/ppermute | solution.py:131
  42.4 0.2 broadcast_select_fusion.1
  42.7 0.1 pad_maximum_fusion.src_ref
  42.7 10.0 %shard_map.94 = f32[8192,256]{1,0:T(8,128)} custom-call(s32[256]{0:T(256)S(1)} %bitcast.21, s32[256]{0:T(256)S(1)} %bitcast.23, s32[1]{0:T(128)} %bitcast.18.cnt_ref, bf16[256,128,128]{2,1,0:T(8,128)(2,1)} %bitcast.25, bf16[2048,256]{1,0:T(8,128)(2,1)S(1)} %pad_maximum_fusion.src_ref), custom_call_target="tpu_custom_call" | custom-call | tf_op jit(solution)/shard_map/pallas_call | solution.py:73
  52.8 4.5 %dynamic-slice_bitcast_fusion = f32[16,256,256]{2,1,0:T(8,128)} fusion(f32[2,16,256,256]{3,2,1,0:T(8,128)} %bitcast.27, s32[]{:T(128)S(6)} %select_n.159), kind=kLoop, calls=%fused_computation.3 | loop fusion | bytes 8388612 | tf_op jit(solution)/shard_map/jit(dynamic_index_in_dim)/squeeze | solution.py:146
  57.3 7.5 %collective-permute-done.3 = f32[16,256,256]{2,1,0:T(8,128)} collective-permute-done((f32[16,256,256]{2,1,0:T(8,128)}, f32[16,256,256]{2,1,0:T(8,128)}, u32[]{:S(2)}, u32[]{:S(2)}) %collective-permute-start.3) | collective-permute-done | bytes 4194336 | tf_op jit(solution)/shard_map/ppermute | solution.py:147
  64.8 4.0 %fusion = bf16[16,256,256]{2,1,0:T(8,128)(2,1)S(1)} fusion(f32[16,256,256]{2,1,0:T(8,128)} %collective-permute-done.3, f32[2,16,256,256]{3,2,1,0:T(8,128)} %bitcast.28, s32[]{:T(128)S(6)} %select_n.158), kind=kLoop, calls=%fused_computation.1 | loop fusion | flops 2097152 | bytes 10485764 | tf_op jit(solution)/shard_map/convert_element_type | solution.py:148
  68.9 63.9 %all_to_all.10 = bf16[16,256,256]{2,1,0:T(8,128)(2,1)S(1)} all-to-all(bf16[16,256,256]{2,1,0:T(8,128)(2,1)S(1)} %fusion), channel_id=1, replica_groups=mesh['row'=8,'colhi'=16,'core'=2] {'colhi'}, dimensions={0} | all-to-all | bytes 4194304 | tf_op jit(solution)/shard_map/all_to_all | solution.py:148
  132.8 0.3 convert_reduce_fusion
  133.1 1.1 multiply_convert_fusion
  134.2 0.0 all-gather.2.cloned.1.call-update
  134.2 1.3 fusion.1
  135.5 1.0 collective-permute-start.4
  136.5 4.0 %collective-permute-done.4 = f32[128,256]{1,0:T(8,128)S(1)} collective-permute-done((f32[128,256]{1,0:T(8,128)S(1)}, f32[128,256]{1,0:T(8,128)S(1)}, u32[]{:S(2)}, u32[]{:S(2)}) %collective-permute-start.4) | collective-permute-done | bytes 131104 | tf_op jit(solution)/shard_map/ppermute | solution.py:114
  140.6 3.3 %collective-permute-start.5 = (f32[64,256]{1,0:T(8,128)S(1)}, f32[64,256]{1,0:T(8,128)S(1)}, u32[]{:S(2)}, u32[]{:S(2)}) collective-permute-start(f32[64,256]{1,0:T(8,128)S(1)} %slice_select_fusion.1), channel_id=1, source_target_pairs={{0,64},{32,96},{64,0},{96,32},{128,192},{160,224},{192,128},{224,1... | collective-permute-start | bytes 196616 | tf_op jit(solution)/shard_map/ppermute | solution.py:114
  143.9 2.6 %collective-permute-done.5 = f32[64,256]{1,0:T(8,128)S(1)} collective-permute-done((f32[64,256]{1,0:T(8,128)S(1)}, f32[64,256]{1,0:T(8,128)S(1)}, u32[]{:S(2)}, u32[]{:S(2)}) %collective-permute-start.5) | collective-permute-done | bytes 65568 | tf_op jit(solution)/shard_map/ppermute | solution.py:114
  146.5 5.9 %collective-permute-start.6 = (f32[32,256]{1,0:T(8,128)S(1)}, f32[32,256]{1,0:T(8,128)S(1)}, u32[]{:S(2)}, u32[]{:S(2)}) collective-permute-start(f32[32,256]{1,0:T(8,128)S(1)} %slice_select_fusion.2), channel_id=1, source_target_pairs={{0,128},{32,160},{64,192},{96,224},{128,0},{160,32},{192,64},{224,... | collective-permute-start | bytes 98312 | tf_op jit(solution)/shard_map/ppermute | solution.py:114
  152.4 2.0 collective-permute-done.6
  154.4 1.2 collective-permute-done.7
  155.7 0.4 collective-permute-start.8
  156.1 3.5 %collective-permute-done.8 = f32[32,256]{1,0:T(8,128)S(1)} collective-permute-done((f32[32,256]{1,0:T(8,128)S(1)}, f32[32,256]{1,0:T(8,128)S(1)}, u32[]{:S(2)}, u32[]{:S(2)}) %collective-permute-start.8) | collective-permute-done | bytes 32800 | tf_op jit(solution)/shard_map/ppermute | solution.py:95
  159.6 1.0 collective-permute-start.9
  160.6 4.1 %collective-permute-done.9 = f32[32,256]{1,0:T(8,128)S(1)} collective-permute-done((f32[32,256]{1,0:T(8,128)S(1)}, f32[32,256]{1,0:T(8,128)S(1)}, u32[]{:S(2)}, u32[]{:S(2)}) %collective-permute-start.9) | collective-permute-done | bytes 32800 | tf_op jit(solution)/shard_map/ppermute | solution.py:95
  164.6 2.6 %collective-permute-start.10 = (f32[32,256]{1,0:T(8,128)S(1)}, f32[32,256]{1,0:T(8,128)S(1)}, u32[]{:S(2)}, u32[]{:S(2)}) collective-permute-start(f32[32,256]{1,0:T(8,128)S(1)} %add.75), channel_id=1, source_target_pairs={{0,8},{2,10},{4,12},{6,14},{8,0},{10,2},{12,4},{14,6},{16,24},{18,... | collective-permute-start | bytes 98312 | tf_op jit(solution)/shard_map/ppermute | solution.py:95
  167.2 2.4 collective-permute-done.10
  169.6 3.4 %collective-permute-start.11 = (f32[32,256]{1,0:T(8,128)S(1)}, f32[32,256]{1,0:T(8,128)S(1)}, u32[]{:S(2)}, u32[]{:S(2)}) collective-permute-start(f32[32,256]{1,0:T(8,128)S(1)} %add.76), channel_id=1, source_target_pairs={{0,16},{2,18},{4,20},{6,22},{8,24},{10,26},{12,28},{14,30},{16,0},... | collective-permute-start | bytes 98312 | tf_op jit(solution)/shard_map/ppermute | solution.py:95
  173.0 2.6 %collective-permute-done.11 = f32[32,256]{1,0:T(8,128)S(1)} collective-permute-done((f32[32,256]{1,0:T(8,128)S(1)}, f32[32,256]{1,0:T(8,128)S(1)}, u32[]{:S(2)}, u32[]{:S(2)}) %collective-permute-start.11) | collective-permute-done | bytes 32800 | tf_op jit(solution)/shard_map/ppermute | solution.py:95
  175.7 5.0 %collective-permute-start.12 = (f32[32,256]{1,0:T(8,128)S(1)}, f32[32,256]{1,0:T(8,128)S(1)}, u32[]{:S(2)}, u32[]{:S(2)}) collective-permute-start(f32[32,256]{1,0:T(8,128)S(1)} %add.77), channel_id=1, source_target_pairs={{0,128},{32,160},{64,192},{96,224},{128,0},{160,32},{192,64},{224,... | collective-permute-start | bytes 98312 | tf_op jit(solution)/shard_map/ppermute | solution.py:119
  180.7 2.8 %collective-permute-done.12 = f32[32,256]{1,0:T(8,128)S(1)} collective-permute-done((f32[32,256]{1,0:T(8,128)S(1)}, f32[32,256]{1,0:T(8,128)S(1)}, u32[]{:S(2)}, u32[]{:S(2)}) %collective-permute-start.12) | collective-permute-done | bytes 32800 | tf_op jit(solution)/shard_map/ppermute | solution.py:119
  183.5 2.7 %collective-permute-start.13 = (f32[64,256]{1,0:T(8,128)S(1)}, f32[64,256]{1,0:T(8,128)S(1)}, u32[]{:S(2)}, u32[]{:S(2)}) collective-permute-start(f32[64,256]{1,0:T(8,128)S(1)} %pad_maximum_fusion.4), channel_id=1, source_target_pairs={{0,64},{32,96},{64,0},{96,32},{128,192},{160,224},{192,128},{224,1... | collective-permute-start | bytes 196616 | tf_op jit(solution)/shard_map/ppermute | solution.py:119
  186.2 3.5 %collective-permute-done.13 = f32[64,256]{1,0:T(8,128)S(1)} collective-permute-done((f32[64,256]{1,0:T(8,128)S(1)}, f32[64,256]{1,0:T(8,128)S(1)}, u32[]{:S(2)}, u32[]{:S(2)}) %collective-permute-start.13) | collective-permute-done | bytes 65568 | tf_op jit(solution)/shard_map/ppermute | solution.py:119
  189.7 1.4 collective-permute-start.14
  191.0 3.7 %collective-permute-done.14 = f32[128,256]{1,0:T(8,128)S(1)} collective-permute-done((f32[128,256]{1,0:T(8,128)S(1)}, f32[128,256]{1,0:T(8,128)S(1)}, u32[]{:S(2)}, u32[]{:S(2)}) %collective-permute-start.14) | collective-permute-done | bytes 131104 | tf_op jit(solution)/shard_map/ppermute | solution.py:119
  194.7 0.7 maximum_multiply_fusion
  195.5 2.8 %all-gather.2.cloned.1.call-done.src_ref = bf16[8192,256]{1,0:T(8,128)(2,1)} async-done(((bf16[256,256]{1,0:T(8,128)(2,1)}), bf16[8192,256]{1,0:T(8,128)(2,1)}) %all-gather.2.cloned.1.call-update) | async-done | bytes 4194320 | tf_op jit(solution)/shard_map/all_gather | solution.py:185
  198.3 2.2 copy-done.1
  200.5 5.3 %shard_map.95 = bf16[2048,256]{1,0:T(8,128)(2,1)S(1)} custom-call(s32[256]{0:T(256)S(1)} %bitcast.22, s32[256]{0:T(256)S(1)} %bitcast.24, s32[1]{0:T(128)} %bitcast.19.cnt_ref, bf16[256,128,128]{2,1,0:T(8,128)(2,1)} %bitcast.26, bf16[8192,256]{1,0:T(8,128)(2,1)S(1)} %copy-done.1), custom_call_target="tpu_custom_call" | custom-call | tf_op jit(solution)/shard_map/pallas_call | solution.py:73
  205.8 37.2 %all_to_all.11 = bf16[8,256,256]{2,1,0:T(8,128)(2,1)S(1)} all-to-all(bf16[8,256,256]{2,1,0:T(8,128)(2,1)S(1)} %bitcast.20), channel_id=1, replica_groups=mesh['row'=8,'colhi'=16,'core'=2] {'row'}, dimensions={0} | all-to-all | bytes 2097152 | tf_op jit(solution)/shard_map/all_to_all | solution.py:85
  243.0 0.1 reduce_sum.22
  243.1 0.9 convolution_convert_fusion
  (29 shorter events, 0.3 us)
Async XLA Ops:
  7.2 125.9 %copy-start = (bf16[256,256]{1,0:T(8,128)(2,1)S(1)}, bf16[256,256]{1,0:T(8,128)(2,1)}, u32[]{:S(2)}) copy-start(bf16[256,256]{1,0:T(8,128)(2,1)} %param.8) | copy-start | bytes 393220
  7.2 35.6 %copy-start.3 = (s32[1,256]{1,0:T(1,128)S(1)}, s32[1,256]{1,0:T(1,128)}, u32[]{:S(2)}) copy-start(s32[1,256]{1,0:T(1,128)} %param.12) | copy-start | bytes 3076
  7.2 35.6 %copy-start.2 = (s32[1,256]{1,0:T(1,128)S(1)}, s32[1,256]{1,0:T(1,128)}, u32[]{:S(2)}) copy-start(s32[1,256]{1,0:T(1,128)} %param.11) | copy-start | bytes 3076
  7.2 191.1 %all-gather.2.cloned.1.call-start = ((), (), s32[]{:S(2)}) async-start(), calls=%async_computation.2 | async-start | bytes 4325376 | tf_op jit(solution)/shard_map/all_gather | solution.py:185
  7.2 5.5 %collective-permute-start = (bf16[256,256]{1,0:T(8,128)(2,1)}, bf16[256,256]{1,0:T(8,128)(2,1)S(1)}, u32[]{:S(2)}, u32[]{:S(2)}) collective-permute-start(bf16[256,256]{1,0:T(8,128)(2,1)} %param.7), channel_id=1, source_target_pairs={{0,32},{32,0},{64,96},{96,64},{128,160},{160,128},{192,224},{224,1... | collective-permute-start | bytes 393224 | tf_op jit(solution)/shard_map/ppermute | solution.py:131
  13.7 8.8 %collective-permute-start.1 = (bf16[512,256]{1,0:T(8,128)(2,1)S(1)}, bf16[512,256]{1,0:T(8,128)(2,1)S(1)}, u32[]{:S(2)}, u32[]{:S(2)}) collective-permute-start(bf16[512,256]{1,0:T(8,128)(2,1)S(1)} %pad_maximum_fusion.2), channel_id=1, source_target_pairs={{0,64},{32,96},{64,0},{96,32},{128,192},{160,224},{192,128},{224,1... | collective-permute-start | bytes 786440 | tf_op jit(solution)/shard_map/ppermute | solution.py:131
  22.7 19.8 %collective-permute-start.2 = (bf16[1024,256]{1,0:T(8,128)(2,1)S(1)}, bf16[1024,256]{1,0:T(8,128)(2,1)S(1)}, u32[]{:S(2)}, u32[]{:S(2)}) collective-permute-start(bf16[1024,256]{1,0:T(8,128)(2,1)S(1)} %pad_maximum_fusion.1), channel_id=1, source_target_pairs={{0,128},{32,160},{64,192},{96,224},{128,0},{160,32},{192,64},{224,... | collective-permute-start | bytes 1572872 | tf_op jit(solution)/shard_map/ppermute | solution.py:131
  57.3 7.5 %collective-permute-start.3 = (f32[16,256,256]{2,1,0:T(8,128)}, f32[16,256,256]{2,1,0:T(8,128)}, u32[]{:S(2)}, u32[]{:S(2)}) collective-permute-start(f32[16,256,256]{2,1,0:T(8,128)} %dynamic-slice_bitcast_fusion), channel_id=1, source_target_pairs={{0,1},{1,0},{2,3},{3,2},{4,5},{5,4},{6,7},{7,6},{8,9},{9,8},{10,11... | collective-permute-start | bytes 12582920 | tf_op jit(solution)/shard_map/ppermute | solution.py:147
  68.9 64.2 %copy-start.4 = (bf16[256,256]{1,0:T(8,128)(2,1)S(1)}, bf16[256,256]{1,0:T(8,128)(2,1)}, u32[]{:S(2)}) copy-start(bf16[256,256]{1,0:T(8,128)(2,1)} %param.9) | copy-start | bytes 393220
  135.5 5.1 %collective-permute-start.4 = (f32[128,256]{1,0:T(8,128)S(1)}, f32[128,256]{1,0:T(8,128)S(1)}, u32[]{:S(2)}, u32[]{:S(2)}) collective-permute-start(f32[128,256]{1,0:T(8,128)S(1)} %slice_select_fusion), channel_id=1, source_target_pairs={{0,32},{32,0},{64,96},{96,64},{128,160},{160,128},{192,224},{224,1... | collective-permute-start | bytes 393224 | tf_op jit(solution)/shard_map/ppermute | solution.py:114
  140.6 5.9 %collective-permute-start.5 = (f32[64,256]{1,0:T(8,128)S(1)}, f32[64,256]{1,0:T(8,128)S(1)}, u32[]{:S(2)}, u32[]{:S(2)}) collective-permute-start(f32[64,256]{1,0:T(8,128)S(1)} %slice_select_fusion.1), channel_id=1, source_target_pairs={{0,64},{32,96},{64,0},{96,32},{128,192},{160,224},{192,128},{224,1... | collective-permute-start | bytes 196616 | tf_op jit(solution)/shard_map/ppermute | solution.py:114
  146.5 7.9 %collective-permute-start.6 = (f32[32,256]{1,0:T(8,128)S(1)}, f32[32,256]{1,0:T(8,128)S(1)}, u32[]{:S(2)}, u32[]{:S(2)}) collective-permute-start(f32[32,256]{1,0:T(8,128)S(1)} %slice_select_fusion.2), channel_id=1, source_target_pairs={{0,128},{32,160},{64,192},{96,224},{128,0},{160,32},{192,64},{224,... | collective-permute-start | bytes 98312 | tf_op jit(solution)/shard_map/ppermute | solution.py:114
  154.4 1.2 collective-permute-start.7
  155.7 3.9 %collective-permute-start.8 = (f32[32,256]{1,0:T(8,128)S(1)}, f32[32,256]{1,0:T(8,128)S(1)}, u32[]{:S(2)}, u32[]{:S(2)}) collective-permute-start(f32[32,256]{1,0:T(8,128)S(1)} %add.73), channel_id=1, source_target_pairs={{0,2},{2,0},{4,6},{6,4},{8,10},{10,8},{12,14},{14,12},{16,18},{18,... | collective-permute-start | bytes 98312 | tf_op jit(solution)/shard_map/ppermute | solution.py:95
  159.6 5.0 %collective-permute-start.9 = (f32[32,256]{1,0:T(8,128)S(1)}, f32[32,256]{1,0:T(8,128)S(1)}, u32[]{:S(2)}, u32[]{:S(2)}) collective-permute-start(f32[32,256]{1,0:T(8,128)S(1)} %add.74), channel_id=1, source_target_pairs={{0,4},{2,6},{4,0},{6,2},{8,12},{10,14},{12,8},{14,10},{16,20},{18,... | collective-permute-start | bytes 98312 | tf_op jit(solution)/shard_map/ppermute | solution.py:95
  164.6 5.0 %collective-permute-start.10 = (f32[32,256]{1,0:T(8,128)S(1)}, f32[32,256]{1,0:T(8,128)S(1)}, u32[]{:S(2)}, u32[]{:S(2)}) collective-permute-start(f32[32,256]{1,0:T(8,128)S(1)} %add.75), channel_id=1, source_target_pairs={{0,8},{2,10},{4,12},{6,14},{8,0},{10,2},{12,4},{14,6},{16,24},{18,... | collective-permute-start | bytes 98312 | tf_op jit(solution)/shard_map/ppermute | solution.py:95
  169.6 6.0 %collective-permute-start.11 = (f32[32,256]{1,0:T(8,128)S(1)}, f32[32,256]{1,0:T(8,128)S(1)}, u32[]{:S(2)}, u32[]{:S(2)}) collective-permute-start(f32[32,256]{1,0:T(8,128)S(1)} %add.76), channel_id=1, source_target_pairs={{0,16},{2,18},{4,20},{6,22},{8,24},{10,26},{12,28},{14,30},{16,0},... | collective-permute-start | bytes 98312 | tf_op jit(solution)/shard_map/ppermute | solution.py:95
  175.7 7.8 %collective-permute-start.12 = (f32[32,256]{1,0:T(8,128)S(1)}, f32[32,256]{1,0:T(8,128)S(1)}, u32[]{:S(2)}, u32[]{:S(2)}) collective-permute-start(f32[32,256]{1,0:T(8,128)S(1)} %add.77), channel_id=1, source_target_pairs={{0,128},{32,160},{64,192},{96,224},{128,0},{160,32},{192,64},{224,... | collective-permute-start | bytes 98312 | tf_op jit(solution)/shard_map/ppermute | solution.py:119
  183.5 6.1 %collective-permute-start.13 = (f32[64,256]{1,0:T(8,128)S(1)}, f32[64,256]{1,0:T(8,128)S(1)}, u32[]{:S(2)}, u32[]{:S(2)}) collective-permute-start(f32[64,256]{1,0:T(8,128)S(1)} %pad_maximum_fusion.4), channel_id=1, source_target_pairs={{0,64},{32,96},{64,0},{96,32},{128,192},{160,224},{192,128},{224,1... | collective-permute-start | bytes 196616 | tf_op jit(solution)/shard_map/ppermute | solution.py:119
  189.7 5.1 %collective-permute-start.14 = (f32[128,256]{1,0:T(8,128)S(1)}, f32[128,256]{1,0:T(8,128)S(1)}, u32[]{:S(2)}, u32[]{:S(2)}) collective-permute-start(f32[128,256]{1,0:T(8,128)S(1)} %pad_maximum_fusion.3), channel_id=1, source_target_pairs={{0,32},{32,0},{64,96},{96,64},{128,160},{160,128},{192,224},{224,1... | collective-permute-start | bytes 393224 | tf_op jit(solution)/shard_map/ppermute | solution.py:119
  198.3 2.2 copy-start.1
Sparse Core Ops, SparseCore 0:
  134.3 63.9 all-gather.1
where the time goes:
time: 253 us; the launch traced here: 251 us
  blocking collectives  101 us (40%)
  waiting for transfers between devices  63.9 us (25%)
  starting transfers between devices  38.9 us (15%)
  Pallas kernels  15.3 us (6%)
  between operations  14.9 us (6%)
  local copies, waits for them, and re-layouts  6.74 us (3%)
  other arithmetic  6.74 us (3%)
  matrix products  3.23 us (1%)
    all_to_all x1, blocking collectives, reduce_pairs_then_blocks(): lax.all_to_all(paired.astype(jnp.bfloat16), outer, 0, 0, tiled=False)  63.9 us
    all_to_all x1, blocking collectives, reduce_blocks(): received = lax.all_to_all(pieces, axis, 0, 0, tiled=False)  37.2 us
    ppermute x3, waiting for transfers between devices, gather_pairs(): other = lax.ppermute(value, axis, [(i, i ^ step) for i in range(size)])  21.2 us
    pallas_call x2, Pallas kernels, tile_product(): pl.pallas_call(kernel, grid_spec=grid_spec, out_shape=jax.ShapeDtypeStruc...  15.3 us
    ppermute x5, waiting for transfers between devices, butterfly_sum(): value = value + lax.ppermute(value, axis, pairs)  13.8 us
    ppermute x3, starting transfers between devices, gather_pairs(): other = lax.ppermute(value, axis, [(i, i ^ step) for i in range(size)])  12.2 us
    ppermute x3, starting transfers between devices, split_sum(): lax.ppermute(send, axis, [(i, i ^ step) for i in range(size)])  10.2 us
    ppermute x3, waiting for transfers between devices, split_sum(): other = lax.ppermute(value, axis, [(i, i ^ step) for i in range(size)])  9.97 us
  transfers between devices with their start and end apart: 16, of which 16 were waited for; matrix products, arithmetic and copies ran while one was open for 1% of the time, Pallas kernels for 0%

commit v1 on v0

--- a/solution.py
+++ b/solution.py
@@ -11,7 +11,7 @@
 
 def tile_product(
     tile_block, row_ids, col_ids, occupied, source, out_rows, transpose, out_dtype,
-    cores=1, dev_tiles=1,
+    cores=1, dev_tiles=1, core_index=None,
 ):
     tile_count, tile_side, _ = tile_block.shape
     feat_width = source.shape[1]
@@ -19,11 +19,15 @@
     row_limit = (src_rows if transpose else out_rows) // tile_side - 1
     col_limit = (out_rows if transpose else src_rows) // tile_side - 1
     steps = tile_count // GROUP
-    out_tiles = out_rows // tile_side
-
-    def kernel(rows_ref, cols_ref, cnt_ref, tiles_ref, src_ref, out_ref, acc_ref):
+    part_rows = out_rows // cores
+    if core_index is None:
+        core_index = jnp.zeros((), jnp.int32)
+
+    def kernel(rows_ref, cols_ref, cnt_ref, me_ref, tiles_ref, src_ref, *refs):
+        out_refs, acc_ref = refs[:cores], refs[cores]
         g = pl.program_id(0)
         cnt = cnt_ref[0]
+        me = me_ref[0]
 
         @pl.when(g == 0)
         def _():
@@ -41,43 +45,47 @@
                     prod = lax.dot_general(
                         a, s, (((0,), (0,)), ((), ())), preferred_element_type=jnp.float32
                     )
+                    sel = 0
                     dst = c
                 else:
                     s = src_ref[pl.ds(pl.multiple_of(c * tile_side, tile_side), tile_side), :]
                     prod = jnp.dot(a, s, preferred_element_type=jnp.float32)
                     dev, part = r // dev_tiles, r % dev_tiles
-                    per_core = out_tiles // dev_tiles // cores
-                    dst = ((dev % cores) * per_core + dev // cores) * dev_tiles + part
+                    sel = (dev % cores - me + cores) % cores
+                    dst = (dev // cores) * dev_tiles + part
                 prod = jnp.where(k < cnt, prod, 0.0)
                 sl = pl.ds(pl.multiple_of(dst * tile_side, tile_side), tile_side)
-                acc_ref[sl, :] += prod
+                acc_ref[sel, sl, :] += prod
 
         @pl.when(g == steps - 1)
         def _():
-            out_ref[...] = acc_ref[...].astype(out_ref.dtype)
-
-    def tile_map(g, rows_ref, cols_ref, cnt_ref):
+            for i in range(cores):
+                out_refs[i][...] = acc_ref[i].astype(out_refs[i].dtype)
+
+    def tile_map(g, rows_ref, cols_ref, cnt_ref, me_ref):
         last = jnp.maximum(cnt_ref[0] - 1, 0) // GROUP
         return (jnp.minimum(g, last), 0, 0)
 
     grid_spec = pltpu.PrefetchScalarGridSpec(
-        num_scalar_prefetch=3,
+        num_scalar_prefetch=4,
         grid=(steps,),
         in_specs=[
             pl.BlockSpec((GROUP, tile_side, tile_side), tile_map),
             pl.BlockSpec((src_rows, feat_width), lambda g, *_: (0, 0)),
         ],
-        out_specs=pl.BlockSpec((out_rows, feat_width), lambda g, *_: (0, 0)),
-        scratch_shapes=[pltpu.VMEM((out_rows, feat_width), jnp.float32)],
+        out_specs=[
+            pl.BlockSpec((part_rows, feat_width), lambda g, *_: (0, 0)) for _ in range(cores)
+        ],
+        scratch_shapes=[pltpu.VMEM((cores, part_rows, feat_width), jnp.float32)],
     )
     return pl.pallas_call(
         kernel,
         grid_spec=grid_spec,
-        out_shape=jax.ShapeDtypeStruct((out_rows, feat_width), out_dtype),
+        out_shape=[jax.ShapeDtypeStruct((part_rows, feat_width), out_dtype) for _ in range(cores)],
         compiler_params=pltpu.CompilerParams(
             dimension_semantics=("arbitrary",), vmem_limit_bytes=48 * 1024 * 1024
         ),
-    )(row_ids, col_ids, occupied.reshape(1), tile_block, source)
+    )(row_ids, col_ids, occupied.reshape(1), core_index.reshape(1).astype(jnp.int32), tile_block, source)
 
 
 def reduce_blocks(partial_value, axis, devices):
@@ -137,13 +145,11 @@
     return value
 
 
-def reduce_pairs_then_blocks(partial_value, outer, inner):
+def reduce_pairs_then_blocks(keep, send, outer, inner):
     outer_size = lax.axis_size(outer)
     inner_size = lax.axis_size(inner)
-    pieces = partial_value.reshape(inner_size, outer_size, -1, partial_value.shape[1])
-    me = lax.axis_index(inner)
-    keep = lax.dynamic_index_in_dim(pieces, me, 0, keepdims=False)
-    send = lax.dynamic_index_in_dim(pieces, inner_size - 1 - me, 0, keepdims=False)
+    keep = keep.reshape(outer_size, -1, keep.shape[1])
+    send = send.reshape(outer_size, -1, send.shape[1])
     paired = keep + lax.ppermute(send, inner, [(i, inner_size - 1 - i) for i in range(inner_size)])
     received = lax.all_to_all(paired.astype(jnp.bfloat16), outer, 0, 0, tiled=False)
     return received.astype(jnp.float32).sum(0)
@@ -166,11 +172,12 @@
     col_ids = tile_cols[0]
     occupied = tile_count[0, 0]
     column_source = gather_pairs(features, "row")
-    partial_value = tile_product(
+    keep, send = tile_product(
         tile_block, row_ids, col_ids, occupied, column_source, col_devices * node_rows, False,
         jnp.float32, cores=lax.axis_size("core"), dev_tiles=node_rows // tile_block.shape[1],
-    )
-    mixed = reduce_pairs_then_blocks(partial_value, "colhi", "core")
+        core_index=lax.axis_index("core"),
+    )
+    mixed = reduce_pairs_then_blocks(keep, send, "colhi", "core")
     pre = jnp.dot(
         mixed, weight.astype(jnp.float32), precision=lax.Precision.HIGHEST,
         preferred_element_type=jnp.float32,
@@ -185,7 +192,7 @@
     row_source = lax.all_gather(grad_pre, col_axes, axis=0, tiled=True)
     row_source, weight_grad = lax.optimization_barrier((row_source, weight_grad))
     output = jax.nn.silu(pre).astype(jnp.bfloat16)
-    back_terms = tile_product(
+    (back_terms,) = tile_product(
         tile_block, row_ids, col_ids, occupied, row_source, row_devices * node_rows, True,
         jnp.bfloat16,
     )

time: 253 us -> 246 us (0.972)
  waiting for transfers between devices: 63.9 us -> 59.3 us
  local copies, waits for them, and re-layouts: 6.74 us -> 2.21 us
  blocking collectives: 101 us -> 105 us
  Pallas kernels: 15.3 us -> 11.4 us
  starting transfers between devices: 38.9 us -> 42.2 us
  other arithmetic: 6.74 us -> 3.71 us
    squeeze x1 -> x0, local copies, waits for them, and re-layouts: 4.53 us -> none  [reduce_pairs_then_blocks(): lax.dynamic_index_in_dim(pieces, inner_size - 1 - me, 0, keepdims=False)]
    pallas_call x2, Pallas kernels: 15.3 us -> 11.4 us  [tile_product(): pl.pallas_call(kernel, grid_spec=grid_spec, out_shape=[jax.ShapeDtypeStru...]
    all_to_all x1, blocking collectives: 63.9 us -> 67.7 us  [reduce_pairs_then_blocks(): lax.all_to_all(paired.astype(jnp.bfloat16), outer, 0, 0, tiled=False)]
    convert_element_type x1, other arithmetic: 4.04 us -> 1.01 us  [reduce_pairs_then_blocks(): paired.astype(jnp.bfloat16)]
where the time goes in v1:
time: 246 us; the launch traced here: 242 us
  blocking collectives  105 us (43%)
  waiting for transfers between devices  59.3 us (24%)
  starting transfers between devices  42.2 us (17%)
  between operations  14.9 us (6%)
  Pallas kernels  11.4 us (5%)
  other arithmetic  3.71 us (2%)
  matrix products  3.23 us (1%)
    all_to_all x1, blocking collectives, reduce_pairs_then_blocks(): lax.all_to_all(paired.astype(jnp.bfloat16), outer, 0, 0, tiled=False)  67.7 us
    all_to_all x1, blocking collectives, reduce_blocks(): received = lax.all_to_all(pieces, axis, 0, 0, tiled=False)  37.6 us
    ppermute x3, waiting for transfers between devices, gather_pairs(): other = lax.ppermute(value, axis, [(i, i ^ step) for i in range(size)])  21.2 us
    ppermute x5, waiting for transfers between devices, butterfly_sum(): value = value + lax.ppermute(value, axis, pairs)  13 us
    ppermute x3, starting transfers between devices, gather_pairs(): other = lax.ppermute(value, axis, [(i, i ^ step) for i in range(size)])  12.2 us
    ppermute x3, starting transfers between devices, split_sum(): lax.ppermute(send, axis, [(i, i ^ step) for i in range(size)])  12 us
    pallas_call x2, Pallas kernels, tile_product(): pl.pallas_call(kernel, grid_spec=grid_spec, out_shape=[jax.ShapeDtypeStru...  11.4 us
    ppermute x3, starting transfers between devices, split_sum(): other = lax.ppermute(value, axis, [(i, i ^ step) for i in range(size)])  10.8 us
  transfers between devices with their start and end apart: 16, of which 16 were waited for; matrix products, arithmetic and copies ran while one was open for 1% of the time, Pallas kernels for 0%

profile of v1, /device:TPU:4, one launch (start us, length us, event | category | flops | bytes accessed | tf_op | source)
XLA Modules:
  0.0 242.2 jit_solution(3352867897303714514)
XLA Ops:
  7.2 0.0 copy-start
  7.2 0.0 all-gather.2.cloned.1.call-start
  7.2 1.7 collective-permute-start
  8.9 3.9 %collective-permute-done = bf16[256,256]{1,0:T(8,128)(2,1)S(1)} collective-permute-done((bf16[256,256]{1,0:T(8,128)(2,1)}, bf16[256,256]{1,0:T(8,128)(2,1)S(1)}, u32[]{:S(2)}, u32[]{:S(2)}) %collective-permute-start) | collective-permute-done | bytes 131104 | tf_op jit(solution)/shard_map/ppermute | solution.py:139
  12.8 0.9 broadcast_select_fusion.5
  13.7 3.3 %collective-permute-start.1 = (bf16[512,256]{1,0:T(8,128)(2,1)S(1)}, bf16[512,256]{1,0:T(8,128)(2,1)S(1)}, u32[]{:S(2)}, u32[]{:S(2)}) collective-permute-start(bf16[512,256]{1,0:T(8,128)(2,1)S(1)} %pad_maximum_fusion.2), channel_id=1, source_target_pairs={{0,64},{32,96},{64,0},{96,32},{128,192},{160,224},{192,128},{224,1... | collective-permute-start | bytes 786440 | tf_op jit(solution)/shard_map/ppermute | solution.py:139
  17.0 5.5 %collective-permute-done.1 = bf16[512,256]{1,0:T(8,128)(2,1)S(1)} collective-permute-done((bf16[512,256]{1,0:T(8,128)(2,1)S(1)}, bf16[512,256]{1,0:T(8,128)(2,1)S(1)}, u32[]{:S(2)}, u32[]{:S(2)}) %collective-permute-start.1) | collective-permute-done | bytes 262176 | tf_op jit(solution)/shard_map/ppermute | solution.py:139
  22.5 0.1 broadcast_select_fusion.3
  22.7 7.3 %collective-permute-start.2 = (bf16[1024,256]{1,0:T(8,128)(2,1)S(1)}, bf16[1024,256]{1,0:T(8,128)(2,1)S(1)}, u32[]{:S(2)}, u32[]{:S(2)}) collective-permute-start(bf16[1024,256]{1,0:T(8,128)(2,1)S(1)} %pad_maximum_fusion.1), channel_id=1, source_target_pairs={{0,128},{32,160},{64,192},{96,224},{128,0},{160,32},{192,64},{224,... | collective-permute-start | bytes 1572872 | tf_op jit(solution)/shard_map/ppermute | solution.py:139
  30.6 11.8 %collective-permute-done.2 = bf16[1024,256]{1,0:T(8,128)(2,1)S(1)} collective-permute-done((bf16[1024,256]{1,0:T(8,128)(2,1)S(1)}, bf16[1024,256]{1,0:T(8,128)(2,1)S(1)}, u32[]{:S(2)}, u32[]{:S(2)}) %collective-permute-start.2) | collective-permute-done | bytes 524320 | tf_op jit(solution)/shard_map/ppermute | solution.py:139
  42.4 0.2 broadcast_select_fusion.1
  42.7 0.1 pad_maximum_fusion.src_ref
  42.7 7.4 %shard_map.94 = (f32[4096,256]{1,0:T(8,128)S(1)}, f32[4096,256]{1,0:T(8,128)}) custom-call(s32[256]{0:T(256)S(1)} %bitcast.18, s32[256]{0:T(256)S(1)} %bitcast.20, s32[1]{0:T(128)} %bitcast.14.cnt_ref, s32[1]{0:T(128)} %bitcast.3.me_ref, bf16[256,128,128]{2,1,0:T(8,128)(2,1)} %bitcast.22, bf16[2048,256]{1,0:T(8,128)(2,1)S(1)} %pad_maximum_fusion.src_ref), custom_call_target="tpu_custom_call" | custom-call | tf_op jit(solution)/shard_map/pallas_call | solution.py:81
  50.2 7.4 %collective-permute-done.3 = f32[16,256,256]{2,1,0:T(8,128)S(1)} collective-permute-done((f32[16,256,256]{2,1,0:T(8,128)}, f32[16,256,256]{2,1,0:T(8,128)S(1)}, u32[]{:S(2)}, u32[]{:S(2)}) %collective-permute-start.3) | collective-permute-done | bytes 4194336 | tf_op jit(solution)/shard_map/ppermute | solution.py:153
  57.6 1.0 add_convert_fusion
  58.6 67.7 %all_to_all.10 = bf16[16,256,256]{2,1,0:T(8,128)(2,1)S(1)} all-to-all(bf16[16,256,256]{2,1,0:T(8,128)(2,1)S(1)} %add_convert_fusion), channel_id=1, replica_groups=mesh['row'=8,'colhi'=16,'core'=2] {'colhi'}, dimensions={0} | all-to-all | bytes 4194304 | tf_op jit(solution)/shard_map/all_to_all | solution.py:154
  126.3 0.3 convert_reduce_fusion
  126.6 1.1 multiply_convert_fusion
  127.6 0.0 all-gather.2.cloned.1.call-update
  127.7 1.3 fusion
  129.0 2.0 collective-permute-start.4
  131.0 3.0 %collective-permute-done.4 = f32[128,256]{1,0:T(8,128)S(1)} collective-permute-done((f32[128,256]{1,0:T(8,128)S(1)}, f32[128,256]{1,0:T(8,128)S(1)}, u32[]{:S(2)}, u32[]{:S(2)}) %collective-permute-start.4) | collective-permute-done | bytes 131104 | tf_op jit(solution)/shard_map/ppermute | solution.py:122
  134.1 3.9 %collective-permute-start.5 = (f32[64,256]{1,0:T(8,128)S(1)}, f32[64,256]{1,0:T(8,128)S(1)}, u32[]{:S(2)}, u32[]{:S(2)}) collective-permute-start(f32[64,256]{1,0:T(8,128)S(1)} %slice_select_fusion.1), channel_id=1, source_target_pairs={{0,64},{32,96},{64,0},{96,32},{128,192},{160,224},{192,128},{224,1... | collective-permute-start | bytes 196616 | tf_op jit(solution)/shard_map/ppermute | solution.py:122
  138.0 2.2 collective-permute-done.5
  140.3 6.1 %collective-permute-start.6 = (f32[32,256]{1,0:T(8,128)S(1)}, f32[32,256]{1,0:T(8,128)S(1)}, u32[]{:S(2)}, u32[]{:S(2)}) collective-permute-start(f32[32,256]{1,0:T(8,128)S(1)} %slice_select_fusion.2), channel_id=1, source_target_pairs={{0,128},{32,160},{64,192},{96,224},{128,0},{160,32},{192,64},{224,... | collective-permute-start | bytes 98312 | tf_op jit(solution)/shard_map/ppermute | solution.py:122
  146.4 1.9 collective-permute-done.6
  148.3 1.2 collective-permute-done.7
  149.5 0.5 collective-permute-start.8
  150.0 3.4 %collective-permute-done.8 = f32[32,256]{1,0:T(8,128)S(1)} collective-permute-done((f32[32,256]{1,0:T(8,128)S(1)}, f32[32,256]{1,0:T(8,128)S(1)}, u32[]{:S(2)}, u32[]{:S(2)}) %collective-permute-start.8) | collective-permute-done | bytes 32800 | tf_op jit(solution)/shard_map/ppermute | solution.py:103
  153.4 1.0 collective-permute-start.9
  154.4 4.1 %collective-permute-done.9 = f32[32,256]{1,0:T(8,128)S(1)} collective-permute-done((f32[32,256]{1,0:T(8,128)S(1)}, f32[32,256]{1,0:T(8,128)S(1)}, u32[]{:S(2)}, u32[]{:S(2)}) %collective-permute-start.9) | collective-permute-done | bytes 32800 | tf_op jit(solution)/shard_map/ppermute | solution.py:103
  158.5 2.1 collective-permute-start.10
  160.6 2.3 collective-permute-done.10
  162.9 3.6 %collective-permute-start.11 = (f32[32,256]{1,0:T(8,128)S(1)}, f32[32,256]{1,0:T(8,128)S(1)}, u32[]{:S(2)}, u32[]{:S(2)}) collective-permute-start(f32[32,256]{1,0:T(8,128)S(1)} %add.66), channel_id=1, source_target_pairs={{0,16},{2,18},{4,20},{6,22},{8,24},{10,26},{12,28},{14,30},{16,0},... | collective-permute-start | bytes 98312 | tf_op jit(solution)/shard_map/ppermute | solution.py:103
  166.5 2.0 collective-permute-done.11
  168.5 6.0 %collective-permute-start.12 = (f32[32,256]{1,0:T(8,128)S(1)}, f32[32,256]{1,0:T(8,128)S(1)}, u32[]{:S(2)}, u32[]{:S(2)}) collective-permute-start(f32[32,256]{1,0:T(8,128)S(1)} %add.67), channel_id=1, source_target_pairs={{0,128},{32,160},{64,192},{96,224},{128,0},{160,32},{192,64},{224,... | collective-permute-start | bytes 98312 | tf_op jit(solution)/shard_map/ppermute | solution.py:127
  174.5 1.9 collective-permute-done.12
  176.4 3.4 %collective-permute-start.13 = (f32[64,256]{1,0:T(8,128)S(1)}, f32[64,256]{1,0:T(8,128)S(1)}, u32[]{:S(2)}, u32[]{:S(2)}) collective-permute-start(f32[64,256]{1,0:T(8,128)S(1)} %pad_maximum_fusion.4), channel_id=1, source_target_pairs={{0,64},{32,96},{64,0},{96,32},{128,192},{160,224},{192,128},{224,1... | collective-permute-start | bytes 196616 | tf_op jit(solution)/shard_map/ppermute | solution.py:127
  179.8 3.1 %collective-permute-done.13 = f32[64,256]{1,0:T(8,128)S(1)} collective-permute-done((f32[64,256]{1,0:T(8,128)S(1)}, f32[64,256]{1,0:T(8,128)S(1)}, u32[]{:S(2)}, u32[]{:S(2)}) %collective-permute-start.13) | collective-permute-done | bytes 65568 | tf_op jit(solution)/shard_map/ppermute | solution.py:127
  183.0 1.4 collective-permute-start.14
  184.4 3.7 %collective-permute-done.14 = f32[128,256]{1,0:T(8,128)S(1)} collective-permute-done((f32[128,256]{1,0:T(8,128)S(1)}, f32[128,256]{1,0:T(8,128)S(1)}, u32[]{:S(2)}, u32[]{:S(2)}) %collective-permute-start.14) | collective-permute-done | bytes 131104 | tf_op jit(solution)/shard_map/ppermute | solution.py:127
  188.1 0.7 maximum_multiply_fusion
  188.8 1.8 all-gather.2.cloned.1.call-done.src_ref
  190.6 2.2 copy-done.1
  192.8 3.9 %shard_map.95 = bf16[2048,256]{1,0:T(8,128)(2,1)S(1)} custom-call(s32[256]{0:T(256)S(1)} %bitcast.19, s32[256]{0:T(256)S(1)} %bitcast.21, s32[1]{0:T(128)} %bitcast.15.cnt_ref, s32[1]{0:T(128)} %constant.95.clone.1.me_ref, bf16[256,128,128]{2,1,0:T(8,128)(2,1)} %bitcast.23, bf16[8192,256]{1,0:T(8,128)(2,1)S(1)} %copy-done.1), custom_call_target="tpu_custom_call" | custom-call | tf_op jit(solution)/shard_map/pallas_call | solution.py:81
  196.7 37.6 %all_to_all.11 = bf16[8,256,256]{2,1,0:T(8,128)(2,1)S(1)} all-to-all(bf16[8,256,256]{2,1,0:T(8,128)(2,1)S(1)} %bitcast.16), channel_id=1, replica_groups=mesh['row'=8,'colhi'=16,'core'=2] {'row'}, dimensions={0} | all-to-all | bytes 2097152 | tf_op jit(solution)/shard_map/all_to_all | solution.py:93
  234.3 0.1 reduce_sum.22
  234.5 0.9 convolution_convert_fusion
  (28 shorter events, 0.2 us)
Async XLA Ops:
  7.2 119.4 %copy-start = (bf16[256,256]{1,0:T(8,128)(2,1)S(1)}, bf16[256,256]{1,0:T(8,128)(2,1)}, u32[]{:S(2)}) copy-start(bf16[256,256]{1,0:T(8,128)(2,1)} %param.8) | copy-start | bytes 393220
  7.2 35.6 %copy-start.3 = (s32[1,256]{1,0:T(1,128)S(1)}, s32[1,256]{1,0:T(1,128)}, u32[]{:S(2)}) copy-start(s32[1,256]{1,0:T(1,128)} %param.12) | copy-start | bytes 3076
  7.2 35.6 %copy-start.2 = (s32[1,256]{1,0:T(1,128)S(1)}, s32[1,256]{1,0:T(1,128)}, u32[]{:S(2)}) copy-start(s32[1,256]{1,0:T(1,128)} %param.11) | copy-start | bytes 3076
  7.2 183.4 %all-gather.2.cloned.1.call-start = ((), (), s32[]{:S(2)}) async-start(), calls=%async_computation.2 | async-start | bytes 4325376 | tf_op jit(solution)/shard_map/all_gather | solution.py:192
  7.2 5.5 %collective-permute-start = (bf16[256,256]{1,0:T(8,128)(2,1)}, bf16[256,256]{1,0:T(8,128)(2,1)S(1)}, u32[]{:S(2)}, u32[]{:S(2)}) collective-permute-start(bf16[256,256]{1,0:T(8,128)(2,1)} %param.7), channel_id=1, source_target_pairs={{0,32},{32,0},{64,96},{96,64},{128,160},{160,128},{192,224},{224,1... | collective-permute-start | bytes 393224 | tf_op jit(solution)/shard_map/ppermute | solution.py:139
  13.7 8.8 %collective-permute-start.1 = (bf16[512,256]{1,0:T(8,128)(2,1)S(1)}, bf16[512,256]{1,0:T(8,128)(2,1)S(1)}, u32[]{:S(2)}, u32[]{:S(2)}) collective-permute-start(bf16[512,256]{1,0:T(8,128)(2,1)S(1)} %pad_maximum_fusion.2), channel_id=1, source_target_pairs={{0,64},{32,96},{64,0},{96,32},{128,192},{160,224},{192,128},{224,1... | collective-permute-start | bytes 786440 | tf_op jit(solution)/shard_map/ppermute | solution.py:139
  22.7 19.8 %collective-permute-start.2 = (bf16[1024,256]{1,0:T(8,128)(2,1)S(1)}, bf16[1024,256]{1,0:T(8,128)(2,1)S(1)}, u32[]{:S(2)}, u32[]{:S(2)}) collective-permute-start(bf16[1024,256]{1,0:T(8,128)(2,1)S(1)} %pad_maximum_fusion.1), channel_id=1, source_target_pairs={{0,128},{32,160},{64,192},{96,224},{128,0},{160,32},{192,64},{224,... | collective-permute-start | bytes 1572872 | tf_op jit(solution)/shard_map/ppermute | solution.py:139
  50.2 7.4 %collective-permute-start.3 = (f32[16,256,256]{2,1,0:T(8,128)}, f32[16,256,256]{2,1,0:T(8,128)S(1)}, u32[]{:S(2)}, u32[]{:S(2)}) collective-permute-start(f32[16,256,256]{2,1,0:T(8,128)} %bitcast.24), channel_id=1, source_target_pairs={{0,1},{1,0},{2,3},{3,2},{4,5},{5,4},{6,7},{7,6},{8,9},{9,8},{10,11... | collective-permute-start | bytes 12582920 | tf_op jit(solution)/shard_map/ppermute | solution.py:153
  58.6 68.0 %copy-start.4 = (bf16[256,256]{1,0:T(8,128)(2,1)S(1)}, bf16[256,256]{1,0:T(8,128)(2,1)}, u32[]{:S(2)}) copy-start(bf16[256,256]{1,0:T(8,128)(2,1)} %param.9) | copy-start | bytes 393220
  129.0 5.1 %collective-permute-start.4 = (f32[128,256]{1,0:T(8,128)S(1)}, f32[128,256]{1,0:T(8,128)S(1)}, u32[]{:S(2)}, u32[]{:S(2)}) collective-permute-start(f32[128,256]{1,0:T(8,128)S(1)} %slice_select_fusion), channel_id=1, source_target_pairs={{0,32},{32,0},{64,96},{96,64},{128,160},{160,128},{192,224},{224,1... | collective-permute-start | bytes 393224 | tf_op jit(solution)/shard_map/ppermute | solution.py:122
  134.1 6.1 %collective-permute-start.5 = (f32[64,256]{1,0:T(8,128)S(1)}, f32[64,256]{1,0:T(8,128)S(1)}, u32[]{:S(2)}, u32[]{:S(2)}) collective-permute-start(f32[64,256]{1,0:T(8,128)S(1)} %slice_select_fusion.1), channel_id=1, source_target_pairs={{0,64},{32,96},{64,0},{96,32},{128,192},{160,224},{192,128},{224,1... | collective-permute-start | bytes 196616 | tf_op jit(solution)/shard_map/ppermute | solution.py:122
  140.3 8.0 %collective-permute-start.6 = (f32[32,256]{1,0:T(8,128)S(1)}, f32[32,256]{1,0:T(8,128)S(1)}, u32[]{:S(2)}, u32[]{:S(2)}) collective-permute-start(f32[32,256]{1,0:T(8,128)S(1)} %slice_select_fusion.2), channel_id=1, source_target_pairs={{0,128},{32,160},{64,192},{96,224},{128,0},{160,32},{192,64},{224,... | collective-permute-start | bytes 98312 | tf_op jit(solution)/shard_map/ppermute | solution.py:122
  148.3 1.2 collective-permute-start.7
  149.5 3.9 %collective-permute-start.8 = (f32[32,256]{1,0:T(8,128)S(1)}, f32[32,256]{1,0:T(8,128)S(1)}, u32[]{:S(2)}, u32[]{:S(2)}) collective-permute-start(f32[32,256]{1,0:T(8,128)S(1)} %add.63), channel_id=1, source_target_pairs={{0,2},{2,0},{4,6},{6,4},{8,10},{10,8},{12,14},{14,12},{16,18},{18,... | collective-permute-start | bytes 98312 | tf_op jit(solution)/shard_map/ppermute | solution.py:103
  153.4 5.1 %collective-permute-start.9 = (f32[32,256]{1,0:T(8,128)S(1)}, f32[32,256]{1,0:T(8,128)S(1)}, u32[]{:S(2)}, u32[]{:S(2)}) collective-permute-start(f32[32,256]{1,0:T(8,128)S(1)} %add.64), channel_id=1, source_target_pairs={{0,4},{2,6},{4,0},{6,2},{8,12},{10,14},{12,8},{14,10},{16,20},{18,... | collective-permute-start | bytes 98312 | tf_op jit(solution)/shard_map/ppermute | solution.py:103
  158.5 4.4 %collective-permute-start.10 = (f32[32,256]{1,0:T(8,128)S(1)}, f32[32,256]{1,0:T(8,128)S(1)}, u32[]{:S(2)}, u32[]{:S(2)}) collective-permute-start(f32[32,256]{1,0:T(8,128)S(1)} %add.65), channel_id=1, source_target_pairs={{0,8},{2,10},{4,12},{6,14},{8,0},{10,2},{12,4},{14,6},{16,24},{18,... | collective-permute-start | bytes 98312 | tf_op jit(solution)/shard_map/ppermute | solution.py:103
  162.9 5.6 %collective-permute-start.11 = (f32[32,256]{1,0:T(8,128)S(1)}, f32[32,256]{1,0:T(8,128)S(1)}, u32[]{:S(2)}, u32[]{:S(2)}) collective-permute-start(f32[32,256]{1,0:T(8,128)S(1)} %add.66), channel_id=1, source_target_pairs={{0,16},{2,18},{4,20},{6,22},{8,24},{10,26},{12,28},{14,30},{16,0},... | collective-permute-start | bytes 98312 | tf_op jit(solution)/shard_map/ppermute | solution.py:103
  168.5 7.9 %collective-permute-start.12 = (f32[32,256]{1,0:T(8,128)S(1)}, f32[32,256]{1,0:T(8,128)S(1)}, u32[]{:S(2)}, u32[]{:S(2)}) collective-permute-start(f32[32,256]{1,0:T(8,128)S(1)} %add.67), channel_id=1, source_target_pairs={{0,128},{32,160},{64,192},{96,224},{128,0},{160,32},{192,64},{224,... | collective-permute-start | bytes 98312 | tf_op jit(solution)/shard_map/ppermute | solution.py:127
  176.4 6.6 %collective-permute-start.13 = (f32[64,256]{1,0:T(8,128)S(1)}, f32[64,256]{1,0:T(8,128)S(1)}, u32[]{:S(2)}, u32[]{:S(2)}) collective-permute-start(f32[64,256]{1,0:T(8,128)S(1)} %pad_maximum_fusion.4), channel_id=1, source_target_pairs={{0,64},{32,96},{64,0},{96,32},{128,192},{160,224},{192,128},{224,1... | collective-permute-start | bytes 196616 | tf_op jit(solution)/shard_map/ppermute | solution.py:127
  183.0 5.1 %collective-permute-start.14 = (f32[128,256]{1,0:T(8,128)S(1)}, f32[128,256]{1,0:T(8,128)S(1)}, u32[]{:S(2)}, u32[]{:S(2)}) collective-permute-start(f32[128,256]{1,0:T(8,128)S(1)} %pad_maximum_fusion.3), channel_id=1, source_target_pairs={{0,32},{32,0},{64,96},{96,64},{128,160},{160,128},{192,224},{224,1... | collective-permute-start | bytes 393224 | tf_op jit(solution)/shard_map/ppermute | solution.py:127
  190.6 2.2 copy-start.1
Sparse Core Ops, SparseCore 0:
  127.8 62.7 all-gather.1

commit v2 on v1

--- a/solution.py
+++ b/solution.py
@@ -11,7 +11,7 @@
 
 def tile_product(
     tile_block, row_ids, col_ids, occupied, source, out_rows, transpose, out_dtype,
-    cores=1, dev_tiles=1, core_index=None,
+    cores=1, dev_tiles=1, core_index=None, src_bits=0,
 ):
     tile_count, tile_side, _ = tile_block.shape
     feat_width = source.shape[1]
@@ -48,6 +48,12 @@
                     sel = 0
                     dst = c
                 else:
+                    src_dev, src_part = c // dev_tiles, c % dev_tiles
+                    flipped = 0
+                    for bit in range(src_bits):
+                        flipped = flipped + ((src_dev // 2**bit) % 2) * 2 ** (src_bits - 1 - bit)
+                    if src_bits:
+                        c = flipped * dev_tiles + src_part
                     s = src_ref[pl.ds(pl.multiple_of(c * tile_side, tile_side), tile_side), :]
                     prod = jnp.dot(a, s, preferred_element_type=jnp.float32)
                     dev, part = r // dev_tiles, r % dev_tiles
@@ -134,14 +140,14 @@
 def gather_pairs(value, axis):
     size = lax.axis_size(axis)
     me = lax.axis_index(axis)
-    step = 1
-    while step < size:
+    step = size // 2
+    while step >= 1:
         other = lax.ppermute(value, axis, [(i, i ^ step) for i in range(size)])
         first = (me // step) % 2 == 0
         value = jnp.concatenate(
             [jnp.where(first, value, other), jnp.where(first, other, value)], axis=0
         )
-        step *= 2
+        step //= 2
     return value
 
 
@@ -175,7 +181,7 @@
     keep, send = tile_product(
         tile_block, row_ids, col_ids, occupied, column_source, col_devices * node_rows, False,
         jnp.float32, cores=lax.axis_size("core"), dev_tiles=node_rows // tile_block.shape[1],
-        core_index=lax.axis_index("core"),
+        core_index=lax.axis_index("core"), src_bits=row_devices.bit_length() - 1,
     )
     mixed = reduce_pairs_then_blocks(keep, send, "colhi", "core")
     pre = jnp.dot(

time: 246 us -> 242 us (0.984)
  blocking collectives: 105 us -> 95.7 us
  Pallas kernels: 11.4 us -> 16.4 us
  waiting for transfers between devices: 59.3 us -> 64.1 us
  starting transfers between devices: 42.2 us -> 38.4 us
    all_to_all x1, blocking collectives: 67.7 us -> 58.2 us  [reduce_pairs_then_blocks(): lax.all_to_all(paired.astype(jnp.bfloat16), outer, 0, 0, tiled=False)]
    pallas_call x2, Pallas kernels: 11.4 us -> 16.4 us  [tile_product(): pl.pallas_call(kernel, grid_spec=grid_spec, out_shape=[jax.ShapeDtypeStru...]
    ppermute x3, waiting for transfers between devices: 7.18 us -> 10.1 us  [split_sum(): lax.ppermute(send, axis, [(i, i ^ step) for i in range(size)])]
where the time goes in v2:
time: 242 us; the launch traced here: 239 us
  blocking collectives  95.7 us (40%)
  waiting for transfers between devices  64.1 us (26%)
  starting transfers between devices  38.4 us (16%)
  Pallas kernels  16.4 us (7%)
  between operations  14.9 us (6%)
  other arithmetic  3.71 us (2%)
  matrix products  3.23 us (1%)
    all_to_all x1, blocking collectives, reduce_pairs_then_blocks(): lax.all_to_all(paired.astype(jnp.bfloat16), outer, 0, 0, tiled=False)  58.2 us
    all_to_all x1, blocking collectives, reduce_blocks(): received = lax.all_to_all(pieces, axis, 0, 0, tiled=False)  37.5 us
    ppermute x3, waiting for transfers between devices, gather_pairs(): other = lax.ppermute(value, axis, [(i, i ^ step) for i in range(size)])  19.4 us
    pallas_call x2, Pallas kernels, tile_product(): pl.pallas_call(kernel, grid_spec=grid_spec, out_shape=[jax.ShapeDtypeStru...  16.4 us
    ppermute x5, waiting for transfers between devices, butterfly_sum(): value = value + lax.ppermute(value, axis, pairs)  14.6 us
    ppermute x3, starting transfers between devices, gather_pairs(): other = lax.ppermute(value, axis, [(i, i ^ step) for i in range(size)])  12.2 us
    ppermute x3, waiting for transfers between devices, split_sum(): other = lax.ppermute(value, axis, [(i, i ^ step) for i in range(size)])  10.5 us
    ppermute x3, starting transfers between devices, split_sum(): lax.ppermute(send, axis, [(i, i ^ step) for i in range(size)])  10.2 us
  transfers between devices with their start and end apart: 16, of which 16 were waited for; matrix products, arithmetic and copies ran while one was open for 1% of the time, Pallas kernels for 0%

profile of v2, /device:TPU:4, one launch (start us, length us, event | category | flops | bytes accessed | tf_op | source)
XLA Modules:
  0.0 238.6 jit_solution(11809425885740919600)
XLA Ops:
  7.2 0.0 all-gather.2.cloned.1.call-start
  7.2 7.3 %collective-permute-start = (bf16[256,256]{1,0:T(8,128)(2,1)}, bf16[256,256]{1,0:T(8,128)(2,1)S(1)}, u32[]{:S(2)}, u32[]{:S(2)}) collective-permute-start(bf16[256,256]{1,0:T(8,128)(2,1)} %param.7), channel_id=1, source_target_pairs={{0,128},{32,160},{64,192},{96,224},{128,0},{160,32},{192,64},{224,... | collective-permute-start | bytes 393224 | tf_op jit(solution)/shard_map/ppermute | solution.py:145
  14.5 3.8 %collective-permute-done = bf16[256,256]{1,0:T(8,128)(2,1)S(1)} collective-permute-done((bf16[256,256]{1,0:T(8,128)(2,1)}, bf16[256,256]{1,0:T(8,128)(2,1)S(1)}, u32[]{:S(2)}, u32[]{:S(2)}) %collective-permute-start) | collective-permute-done | bytes 131104 | tf_op jit(solution)/shard_map/ppermute | solution.py:145
  18.3 0.9 broadcast_select_fusion.5
  19.3 3.3 %collective-permute-start.1 = (bf16[512,256]{1,0:T(8,128)(2,1)S(1)}, bf16[512,256]{1,0:T(8,128)(2,1)S(1)}, u32[]{:S(2)}, u32[]{:S(2)}) collective-permute-start(bf16[512,256]{1,0:T(8,128)(2,1)S(1)} %pad_maximum_fusion.2), channel_id=1, source_target_pairs={{0,64},{32,96},{64,0},{96,32},{128,192},{160,224},{192,128},{224,1... | collective-permute-start | bytes 786440 | tf_op jit(solution)/shard_map/ppermute | solution.py:145
  22.6 5.7 %collective-permute-done.1 = bf16[512,256]{1,0:T(8,128)(2,1)S(1)} collective-permute-done((bf16[512,256]{1,0:T(8,128)(2,1)S(1)}, bf16[512,256]{1,0:T(8,128)(2,1)S(1)}, u32[]{:S(2)}, u32[]{:S(2)}) %collective-permute-start.1) | collective-permute-done | bytes 262176 | tf_op jit(solution)/shard_map/ppermute | solution.py:145
  28.2 0.1 broadcast_select_fusion.3
  28.4 1.7 collective-permute-start.2
  30.7 9.9 %collective-permute-done.2 = bf16[1024,256]{1,0:T(8,128)(2,1)S(1)} collective-permute-done((bf16[1024,256]{1,0:T(8,128)(2,1)S(1)}, bf16[1024,256]{1,0:T(8,128)(2,1)S(1)}, u32[]{:S(2)}, u32[]{:S(2)}) %collective-permute-start.2) | collective-permute-done | bytes 524320 | tf_op jit(solution)/shard_map/ppermute | solution.py:145
  40.6 0.2 broadcast_select_fusion.1
  40.8 0.1 pad_maximum_fusion.src_ref
  40.9 11.1 %shard_map.94 = (f32[4096,256]{1,0:T(8,128)S(1)}, f32[4096,256]{1,0:T(8,128)}) custom-call(s32[256]{0:T(256)S(1)} %bitcast.18, s32[256]{0:T(256)S(1)} %bitcast.20, s32[1]{0:T(128)} %bitcast.14.cnt_ref, s32[1]{0:T(128)} %bitcast.3.me_ref, bf16[256,128,128]{2,1,0:T(8,128)(2,1)} %bitcast.22, bf16[2048,256]{1,0:T(8,128)(2,1)S(1)} %pad_maximum_fusion.src_ref), custom_call_target="tpu_custom_call" | custom-call | tf_op jit(solution)/shard_map/pallas_call | solution.py:87
  52.1 0.3 collective-permute-start.3
  52.4 7.0 %collective-permute-done.3 = f32[16,256,256]{2,1,0:T(8,128)S(1)} collective-permute-done((f32[16,256,256]{2,1,0:T(8,128)}, f32[16,256,256]{2,1,0:T(8,128)S(1)}, u32[]{:S(2)}, u32[]{:S(2)}) %collective-permute-start.3) | collective-permute-done | bytes 4194336 | tf_op jit(solution)/shard_map/ppermute | solution.py:159
  59.4 1.0 add_convert_fusion
  60.4 58.2 %all_to_all.10 = bf16[16,256,256]{2,1,0:T(8,128)(2,1)S(1)} all-to-all(bf16[16,256,256]{2,1,0:T(8,128)(2,1)S(1)} %add_convert_fusion), channel_id=1, replica_groups=mesh['row'=8,'colhi'=16,'core'=2] {'colhi'}, dimensions={0} | all-to-all | bytes 4194304 | tf_op jit(solution)/shard_map/all_to_all | solution.py:160
  118.6 0.3 convert_reduce_fusion
  119.0 1.1 multiply_convert_fusion
  120.0 0.0 all-gather.2.cloned.1.call-update
  120.0 1.3 fusion
  121.4 3.2 %collective-permute-start.4 = (f32[128,256]{1,0:T(8,128)S(1)}, f32[128,256]{1,0:T(8,128)S(1)}, u32[]{:S(2)}, u32[]{:S(2)}) collective-permute-start(f32[128,256]{1,0:T(8,128)S(1)} %slice_select_fusion), channel_id=1, source_target_pairs={{0,32},{32,0},{64,96},{96,64},{128,160},{160,128},{192,224},{224,1... | collective-permute-start | bytes 393224 | tf_op jit(solution)/shard_map/ppermute | solution.py:128
  124.6 3.1 %collective-permute-done.4 = f32[128,256]{1,0:T(8,128)S(1)} collective-permute-done((f32[128,256]{1,0:T(8,128)S(1)}, f32[128,256]{1,0:T(8,128)S(1)}, u32[]{:S(2)}, u32[]{:S(2)}) %collective-permute-start.4) | collective-permute-done | bytes 131104 | tf_op jit(solution)/shard_map/ppermute | solution.py:128
  127.7 0.7 collective-permute-start.5
  128.4 5.1 %collective-permute-done.5 = f32[64,256]{1,0:T(8,128)S(1)} collective-permute-done((f32[64,256]{1,0:T(8,128)S(1)}, f32[64,256]{1,0:T(8,128)S(1)}, u32[]{:S(2)}, u32[]{:S(2)}) %collective-permute-start.5) | collective-permute-done | bytes 65568 | tf_op jit(solution)/shard_map/ppermute | solution.py:128
  133.6 6.3 %collective-permute-start.6 = (f32[32,256]{1,0:T(8,128)S(1)}, f32[32,256]{1,0:T(8,128)S(1)}, u32[]{:S(2)}, u32[]{:S(2)}) collective-permute-start(f32[32,256]{1,0:T(8,128)S(1)} %slice_select_fusion.2), channel_id=1, source_target_pairs={{0,128},{32,160},{64,192},{96,224},{128,0},{160,32},{192,64},{224,... | collective-permute-start | bytes 98312 | tf_op jit(solution)/shard_map/ppermute | solution.py:128
  139.8 1.9 collective-permute-done.6
  141.8 1.2 collective-permute-done.7
  143.0 0.5 collective-permute-start.8
  143.5 3.4 %collective-permute-done.8 = f32[32,256]{1,0:T(8,128)S(1)} collective-permute-done((f32[32,256]{1,0:T(8,128)S(1)}, f32[32,256]{1,0:T(8,128)S(1)}, u32[]{:S(2)}, u32[]{:S(2)}) %collective-permute-start.8) | collective-permute-done | bytes 32800 | tf_op jit(solution)/shard_map/ppermute | solution.py:109
  146.9 1.3 collective-permute-start.9
  148.2 3.8 %collective-permute-done.9 = f32[32,256]{1,0:T(8,128)S(1)} collective-permute-done((f32[32,256]{1,0:T(8,128)S(1)}, f32[32,256]{1,0:T(8,128)S(1)}, u32[]{:S(2)}, u32[]{:S(2)}) %collective-permute-start.9) | collective-permute-done | bytes 32800 | tf_op jit(solution)/shard_map/ppermute | solution.py:109
  152.0 2.7 %collective-permute-start.10 = (f32[32,256]{1,0:T(8,128)S(1)}, f32[32,256]{1,0:T(8,128)S(1)}, u32[]{:S(2)}, u32[]{:S(2)}) collective-permute-start(f32[32,256]{1,0:T(8,128)S(1)} %add.65), channel_id=1, source_target_pairs={{0,8},{2,10},{4,12},{6,14},{8,0},{10,2},{12,4},{14,6},{16,24},{18,... | collective-permute-start | bytes 98312 | tf_op jit(solution)/shard_map/ppermute | solution.py:109
  154.7 2.3 collective-permute-done.10
  157.1 2.3 collective-permute-start.11
  159.4 3.8 %collective-permute-done.11 = f32[32,256]{1,0:T(8,128)S(1)} collective-permute-done((f32[32,256]{1,0:T(8,128)S(1)}, f32[32,256]{1,0:T(8,128)S(1)}, u32[]{:S(2)}, u32[]{:S(2)}) %collective-permute-start.11) | collective-permute-done | bytes 32800 | tf_op jit(solution)/shard_map/ppermute | solution.py:109
  163.2 5.1 %collective-permute-start.12 = (f32[32,256]{1,0:T(8,128)S(1)}, f32[32,256]{1,0:T(8,128)S(1)}, u32[]{:S(2)}, u32[]{:S(2)}) collective-permute-start(f32[32,256]{1,0:T(8,128)S(1)} %add.67), channel_id=1, source_target_pairs={{0,128},{32,160},{64,192},{96,224},{128,0},{160,32},{192,64},{224,... | collective-permute-start | bytes 98312 | tf_op jit(solution)/shard_map/ppermute | solution.py:133
  168.3 2.7 %collective-permute-done.12 = f32[32,256]{1,0:T(8,128)S(1)} collective-permute-done((f32[32,256]{1,0:T(8,128)S(1)}, f32[32,256]{1,0:T(8,128)S(1)}, u32[]{:S(2)}, u32[]{:S(2)}) %collective-permute-start.12) | collective-permute-done | bytes 32800 | tf_op jit(solution)/shard_map/ppermute | solution.py:133
  171.0 2.4 %collective-permute-start.13 = (f32[64,256]{1,0:T(8,128)S(1)}, f32[64,256]{1,0:T(8,128)S(1)}, u32[]{:S(2)}, u32[]{:S(2)}) collective-permute-start(f32[64,256]{1,0:T(8,128)S(1)} %pad_maximum_fusion.4), channel_id=1, source_target_pairs={{0,64},{32,96},{64,0},{96,32},{128,192},{160,224},{192,128},{224,1... | collective-permute-start | bytes 196616 | tf_op jit(solution)/shard_map/ppermute | solution.py:133
  173.5 4.0 %collective-permute-done.13 = f32[64,256]{1,0:T(8,128)S(1)} collective-permute-done((f32[64,256]{1,0:T(8,128)S(1)}, f32[64,256]{1,0:T(8,128)S(1)}, u32[]{:S(2)}, u32[]{:S(2)}) %collective-permute-start.13) | collective-permute-done | bytes 65568 | tf_op jit(solution)/shard_map/ppermute | solution.py:133
  177.5 1.2 collective-permute-start.14
  178.7 3.8 %collective-permute-done.14 = f32[128,256]{1,0:T(8,128)S(1)} collective-permute-done((f32[128,256]{1,0:T(8,128)S(1)}, f32[128,256]{1,0:T(8,128)S(1)}, u32[]{:S(2)}, u32[]{:S(2)}) %collective-permute-start.14) | collective-permute-done | bytes 131104 | tf_op jit(solution)/shard_map/ppermute | solution.py:133
  182.6 0.7 maximum_multiply_fusion
  183.3 2.4 %all-gather.2.cloned.1.call-done.src_ref = bf16[8192,256]{1,0:T(8,128)(2,1)} async-done(((bf16[256,256]{1,0:T(8,128)(2,1)}), bf16[8192,256]{1,0:T(8,128)(2,1)}) %all-gather.2.cloned.1.call-update) | async-done | bytes 4194320 | tf_op jit(solution)/shard_map/all_gather | solution.py:198
  185.7 2.2 copy-done.1
  187.9 5.3 %shard_map.95 = bf16[2048,256]{1,0:T(8,128)(2,1)S(1)} custom-call(s32[256]{0:T(256)S(1)} %bitcast.19, s32[256]{0:T(256)S(1)} %bitcast.21, s32[1]{0:T(128)} %bitcast.15.cnt_ref, s32[1]{0:T(128)} %constant.95.clone.1.me_ref, bf16[256,128,128]{2,1,0:T(8,128)(2,1)} %bitcast.23, bf16[8192,256]{1,0:T(8,128)(2,1)S(1)} %copy-done.1), custom_call_target="tpu_custom_call" | custom-call | tf_op jit(solution)/shard_map/pallas_call | solution.py:87
  193.3 37.5 %all_to_all.11 = bf16[8,256,256]{2,1,0:T(8,128)(2,1)S(1)} all-to-all(bf16[8,256,256]{2,1,0:T(8,128)(2,1)S(1)} %bitcast.16), channel_id=1, replica_groups=mesh['row'=8,'colhi'=16,'core'=2] {'row'}, dimensions={0} | all-to-all | bytes 2097152 | tf_op jit(solution)/shard_map/all_to_all | solution.py:99
  230.7 0.1 reduce_sum.22
  230.9 0.9 convolution_convert_fusion
  (28 shorter events, 0.2 us)
Async XLA Ops:
  7.2 111.8 %copy-start = (bf16[256,256]{1,0:T(8,128)(2,1)S(1)}, bf16[256,256]{1,0:T(8,128)(2,1)}, u32[]{:S(2)}) copy-start(bf16[256,256]{1,0:T(8,128)(2,1)} %param.8) | copy-start | bytes 393220
  7.2 33.7 %copy-start.3 = (s32[1,256]{1,0:T(1,128)S(1)}, s32[1,256]{1,0:T(1,128)}, u32[]{:S(2)}) copy-start(s32[1,256]{1,0:T(1,128)} %param.12) | copy-start | bytes 3076
  7.2 33.7 %copy-start.2 = (s32[1,256]{1,0:T(1,128)S(1)}, s32[1,256]{1,0:T(1,128)}, u32[]{:S(2)}) copy-start(s32[1,256]{1,0:T(1,128)} %param.11) | copy-start | bytes 3076
  7.2 178.5 %all-gather.2.cloned.1.call-start = ((), (), s32[]{:S(2)}) async-start(), calls=%async_computation.2 | async-start | bytes 4325376 | tf_op jit(solution)/shard_map/all_gather | solution.py:198
  7.2 11.1 %collective-permute-start = (bf16[256,256]{1,0:T(8,128)(2,1)}, bf16[256,256]{1,0:T(8,128)(2,1)S(1)}, u32[]{:S(2)}, u32[]{:S(2)}) collective-permute-start(bf16[256,256]{1,0:T(8,128)(2,1)} %param.7), channel_id=1, source_target_pairs={{0,128},{32,160},{64,192},{96,224},{128,0},{160,32},{192,64},{224,... | collective-permute-start | bytes 393224 | tf_op jit(solution)/shard_map/ppermute | solution.py:145
  19.3 9.0 %collective-permute-start.1 = (bf16[512,256]{1,0:T(8,128)(2,1)S(1)}, bf16[512,256]{1,0:T(8,128)(2,1)S(1)}, u32[]{:S(2)}, u32[]{:S(2)}) collective-permute-start(bf16[512,256]{1,0:T(8,128)(2,1)S(1)} %pad_maximum_fusion.2), channel_id=1, source_target_pairs={{0,64},{32,96},{64,0},{96,32},{128,192},{160,224},{192,128},{224,1... | collective-permute-start | bytes 786440 | tf_op jit(solution)/shard_map/ppermute | solution.py:145
  28.4 12.2 %collective-permute-start.2 = (bf16[1024,256]{1,0:T(8,128)(2,1)S(1)}, bf16[1024,256]{1,0:T(8,128)(2,1)S(1)}, u32[]{:S(2)}, u32[]{:S(2)}) collective-permute-start(bf16[1024,256]{1,0:T(8,128)(2,1)S(1)} %pad_maximum_fusion.1), channel_id=1, source_target_pairs={{0,32},{32,0},{64,96},{96,64},{128,160},{160,128},{192,224},{224,1... | collective-permute-start | bytes 1572872 | tf_op jit(solution)/shard_map/ppermute | solution.py:145
  52.1 7.4 %collective-permute-start.3 = (f32[16,256,256]{2,1,0:T(8,128)}, f32[16,256,256]{2,1,0:T(8,128)S(1)}, u32[]{:S(2)}, u32[]{:S(2)}) collective-permute-start(f32[16,256,256]{2,1,0:T(8,128)} %bitcast.24), channel_id=1, source_target_pairs={{0,1},{1,0},{2,3},{3,2},{4,5},{5,4},{6,7},{7,6},{8,9},{9,8},{10,11... | collective-permute-start | bytes 12582920 | tf_op jit(solution)/shard_map/ppermute | solution.py:159
  60.4 58.5 %copy-start.4 = (bf16[256,256]{1,0:T(8,128)(2,1)S(1)}, bf16[256,256]{1,0:T(8,128)(2,1)}, u32[]{:S(2)}) copy-start(bf16[256,256]{1,0:T(8,128)(2,1)} %param.9) | copy-start | bytes 393220
  121.4 6.3 %collective-permute-start.4 = (f32[128,256]{1,0:T(8,128)S(1)}, f32[128,256]{1,0:T(8,128)S(1)}, u32[]{:S(2)}, u32[]{:S(2)}) collective-permute-start(f32[128,256]{1,0:T(8,128)S(1)} %slice_select_fusion), channel_id=1, source_target_pairs={{0,32},{32,0},{64,96},{96,64},{128,160},{160,128},{192,224},{224,1... | collective-permute-start | bytes 393224 | tf_op jit(solution)/shard_map/ppermute | solution.py:128
  127.7 5.9 %collective-permute-start.5 = (f32[64,256]{1,0:T(8,128)S(1)}, f32[64,256]{1,0:T(8,128)S(1)}, u32[]{:S(2)}, u32[]{:S(2)}) collective-permute-start(f32[64,256]{1,0:T(8,128)S(1)} %slice_select_fusion.1), channel_id=1, source_target_pairs={{0,64},{32,96},{64,0},{96,32},{128,192},{160,224},{192,128},{224,1... | collective-permute-start | bytes 196616 | tf_op jit(solution)/shard_map/ppermute | solution.py:128
  133.6 8.2 %collective-permute-start.6 = (f32[32,256]{1,0:T(8,128)S(1)}, f32[32,256]{1,0:T(8,128)S(1)}, u32[]{:S(2)}, u32[]{:S(2)}) collective-permute-start(f32[32,256]{1,0:T(8,128)S(1)} %slice_select_fusion.2), channel_id=1, source_target_pairs={{0,128},{32,160},{64,192},{96,224},{128,0},{160,32},{192,64},{224,... | collective-permute-start | bytes 98312 | tf_op jit(solution)/shard_map/ppermute | solution.py:128
  141.8 1.2 collective-permute-start.7
  143.0 3.9 %collective-permute-start.8 = (f32[32,256]{1,0:T(8,128)S(1)}, f32[32,256]{1,0:T(8,128)S(1)}, u32[]{:S(2)}, u32[]{:S(2)}) collective-permute-start(f32[32,256]{1,0:T(8,128)S(1)} %add.63), channel_id=1, source_target_pairs={{0,2},{2,0},{4,6},{6,4},{8,10},{10,8},{12,14},{14,12},{16,18},{18,... | collective-permute-start | bytes 98312 | tf_op jit(solution)/shard_map/ppermute | solution.py:109
  146.9 5.1 %collective-permute-start.9 = (f32[32,256]{1,0:T(8,128)S(1)}, f32[32,256]{1,0:T(8,128)S(1)}, u32[]{:S(2)}, u32[]{:S(2)}) collective-permute-start(f32[32,256]{1,0:T(8,128)S(1)} %add.64), channel_id=1, source_target_pairs={{0,4},{2,6},{4,0},{6,2},{8,12},{10,14},{12,8},{14,10},{16,20},{18,... | collective-permute-start | bytes 98312 | tf_op jit(solution)/shard_map/ppermute | solution.py:109
  152.0 5.1 %collective-permute-start.10 = (f32[32,256]{1,0:T(8,128)S(1)}, f32[32,256]{1,0:T(8,128)S(1)}, u32[]{:S(2)}, u32[]{:S(2)}) collective-permute-start(f32[32,256]{1,0:T(8,128)S(1)} %add.65), channel_id=1, source_target_pairs={{0,8},{2,10},{4,12},{6,14},{8,0},{10,2},{12,4},{14,6},{16,24},{18,... | collective-permute-start | bytes 98312 | tf_op jit(solution)/shard_map/ppermute | solution.py:109
  157.1 6.1 %collective-permute-start.11 = (f32[32,256]{1,0:T(8,128)S(1)}, f32[32,256]{1,0:T(8,128)S(1)}, u32[]{:S(2)}, u32[]{:S(2)}) collective-permute-start(f32[32,256]{1,0:T(8,128)S(1)} %add.66), channel_id=1, source_target_pairs={{0,16},{2,18},{4,20},{6,22},{8,24},{10,26},{12,28},{14,30},{16,0},... | collective-permute-start | bytes 98312 | tf_op jit(solution)/shard_map/ppermute | solution.py:109
  163.2 7.8 %collective-permute-start.12 = (f32[32,256]{1,0:T(8,128)S(1)}, f32[32,256]{1,0:T(8,128)S(1)}, u32[]{:S(2)}, u32[]{:S(2)}) collective-permute-start(f32[32,256]{1,0:T(8,128)S(1)} %add.67), channel_id=1, source_target_pairs={{0,128},{32,160},{64,192},{96,224},{128,0},{160,32},{192,64},{224,... | collective-permute-start | bytes 98312 | tf_op jit(solution)/shard_map/ppermute | solution.py:133
  171.0 6.4 %collective-permute-start.13 = (f32[64,256]{1,0:T(8,128)S(1)}, f32[64,256]{1,0:T(8,128)S(1)}, u32[]{:S(2)}, u32[]{:S(2)}) collective-permute-start(f32[64,256]{1,0:T(8,128)S(1)} %pad_maximum_fusion.4), channel_id=1, source_target_pairs={{0,64},{32,96},{64,0},{96,32},{128,192},{160,224},{192,128},{224,1... | collective-permute-start | bytes 196616 | tf_op jit(solution)/shard_map/ppermute | solution.py:133
  177.5 5.1 %collective-permute-start.14 = (f32[128,256]{1,0:T(8,128)S(1)}, f32[128,256]{1,0:T(8,128)S(1)}, u32[]{:S(2)}, u32[]{:S(2)}) collective-permute-start(f32[128,256]{1,0:T(8,128)S(1)} %pad_maximum_fusion.3), channel_id=1, source_target_pairs={{0,32},{32,0},{64,96},{96,64},{128,160},{160,128},{192,224},{224,1... | collective-permute-start | bytes 393224 | tf_op jit(solution)/shard_map/ppermute | solution.py:133
  185.7 2.2 copy-start.1
Sparse Core Ops, SparseCore 0:
  120.2 65.5 all-gather.1

commit v3 on v2

--- a/solution.py
+++ b/solution.py
@@ -11,7 +11,7 @@
 
 def tile_product(
     tile_block, row_ids, col_ids, occupied, source, out_rows, transpose, out_dtype,
-    cores=1, dev_tiles=1, core_index=None, src_bits=0,
+    cores=1, dev_tiles=1, core_index=None, src_bits=0, dst_bits=0,
 ):
     tile_count, tile_side, _ = tile_block.shape
     feat_width = source.shape[1]
@@ -46,7 +46,11 @@
                         a, s, (((0,), (0,)), ((), ())), preferred_element_type=jnp.float32
                     )
                     sel = 0
-                    dst = c
+                    dst_dev, dst_part = c // dev_tiles, c % dev_tiles
+                    flipped = 0
+                    for bit in range(dst_bits):
+                        flipped = flipped + ((dst_dev // 2**bit) % 2) * 2 ** (dst_bits - 1 - bit)
+                    dst = flipped * dev_tiles + dst_part if dst_bits else c
                 else:
                     src_dev, src_part = c // dev_tiles, c % dev_tiles
                     flipped = 0
@@ -137,6 +141,21 @@
     return value
 
 
+def halving_sum(value, axis):
+    size = lax.axis_size(axis)
+    me = lax.axis_index(axis)
+    step = 1
+    while step < size:
+        low = (me // step) % 2 == 0
+        half = value.shape[0] // 2
+        head, tail = value[:half], value[half:]
+        send = jnp.where(low, tail, head)
+        keep = jnp.where(low, head, tail)
+        value = keep + lax.ppermute(send, axis, [(i, i ^ step) for i in range(size)])
+        step *= 2
+    return value
+
+
 def gather_pairs(value, axis):
     size = lax.axis_size(axis)
     me = lax.axis_index(axis)
@@ -200,9 +219,10 @@
     output = jax.nn.silu(pre).astype(jnp.bfloat16)
     (back_terms,) = tile_product(
         tile_block, row_ids, col_ids, occupied, row_source, row_devices * node_rows, True,
-        jnp.bfloat16,
-    )
-    aggregated = reduce_blocks(back_terms, "row", row_devices)
+        jnp.float32, dev_tiles=node_rows // tile_block.shape[1],
+        dst_bits=row_devices.bit_length() - 1,
+    )
+    aggregated = halving_sum(back_terms, "row")
     node_grad = aggregated.astype(jnp.bfloat16)
     feature_grad = jnp.dot(node_grad, weight.T, preferred_element_type=jnp.float32).astype(
         jnp.bfloat16

time: 242 us -> 265 us (1.095)
  waiting for transfers between devices: 64.1 us -> 110 us
  blocking collectives: 95.7 us -> 59.3 us
  starting transfers between devices: 38.4 us -> 51.2 us
  Pallas kernels: 16.4 us -> 19.4 us
    ppermute x0 -> x3, waiting for transfers between devices: none -> 50.9 us  [halving_sum(): lax.ppermute(send, axis, [(i, i ^ step) for i in range(size)])]
    all_to_all x1 -> x0, blocking collectives: 37.5 us -> none  [reduce_blocks(): received = lax.all_to_all(pieces, axis, 0, 0, tiled=False)]
    ppermute x0 -> x3, starting transfers between devices: none -> 7.26 us  [halving_sum(): lax.ppermute(send, axis, [(i, i ^ step) for i in range(size)])]
    ppermute x3, waiting for transfers between devices: 10.5 us -> 7.12 us  [split_sum(): other = lax.ppermute(value, axis, [(i, i ^ step) for i in range(size)])]
    pallas_call x2, Pallas kernels: 16.4 us -> 19.4 us  [tile_product(): pl.pallas_call(kernel, grid_spec=grid_spec, out_shape=[jax.ShapeDtypeStru...]
    ppermute x3, starting transfers between devices: 8.76 us -> 11.6 us  [split_sum(): other = lax.ppermute(value, axis, [(i, i ^ step) for i in range(size)])]
  transfers between devices with their start and end apart: 16 -> 19, of which waited for: 16 -> 19; matrix products, arithmetic and copies ran while one was open for 1% -> 1% of each run, Pallas kernels for 0% -> 0%
where the time goes in v3:
time: 265 us; the launch traced here: 263 us
  waiting for transfers between devices  110 us (42%)
  blocking collectives  59.3 us (22%)
  starting transfers between devices  51.2 us (19%)
  Pallas kernels  19.4 us (7%)
  between operations  14.9 us (6%)
  other arithmetic  3.9 us (1%)
  matrix products  3.25 us (1%)
    all_to_all x1, blocking collectives, reduce_pairs_then_blocks(): lax.all_to_all(paired.astype(jnp.bfloat16), outer, 0, 0, tiled=False)  59.3 us
    ppermute x3, waiting for transfers between devices, halving_sum(): lax.ppermute(send, axis, [(i, i ^ step) for i in range(size)])  50.9 us
    pallas_call x2, Pallas kernels, tile_product(): pl.pallas_call(kernel, grid_spec=grid_spec, out_shape=[jax.ShapeDtypeStru...  19.4 us
    ppermute x3, waiting for transfers between devices, gather_pairs(): other = lax.ppermute(value, axis, [(i, i ^ step) for i in range(size)])  19.4 us
    ppermute x5, waiting for transfers between devices, butterfly_sum(): value = value + lax.ppermute(value, axis, pairs)  13.2 us
    ppermute x3, starting transfers between devices, split_sum(): lax.ppermute(send, axis, [(i, i ^ step) for i in range(size)])  12.3 us
    ppermute x3, starting transfers between devices, gather_pairs(): other = lax.ppermute(value, axis, [(i, i ^ step) for i in range(size)])  12.2 us
    ppermute x3, starting transfers between devices, split_sum(): other = lax.ppermute(value, axis, [(i, i ^ step) for i in range(size)])  11.6 us
  transfers between devices with their start and end apart: 19, of which 19 were waited for; matrix products, arithmetic and copies ran while one was open for 1% of the time, Pallas kernels for 0%

profile of v3, /device:TPU:4, one launch (start us, length us, event | category | flops | bytes accessed | tf_op | source)
XLA Modules:
  0.0 262.6 jit_solution(7495079508150215298)
XLA Ops:
  7.2 7.3 %collective-permute-start = (bf16[256,256]{1,0:T(8,128)(2,1)}, bf16[256,256]{1,0:T(8,128)(2,1)S(1)}, u32[]{:S(2)}, u32[]{:S(2)}) collective-permute-start(bf16[256,256]{1,0:T(8,128)(2,1)} %param.7), channel_id=1, source_target_pairs={{0,128},{32,160},{64,192},{96,224},{128,0},{160,32},{192,64},{224,... | collective-permute-start | bytes 393224 | tf_op jit(solution)/shard_map/ppermute | solution.py:164
  14.5 3.8 %collective-permute-done = bf16[256,256]{1,0:T(8,128)(2,1)S(1)} collective-permute-done((bf16[256,256]{1,0:T(8,128)(2,1)}, bf16[256,256]{1,0:T(8,128)(2,1)S(1)}, u32[]{:S(2)}, u32[]{:S(2)}) %collective-permute-start) | collective-permute-done | bytes 131104 | tf_op jit(solution)/shard_map/ppermute | solution.py:164
  18.3 0.9 broadcast_select_fusion.5
  19.3 3.3 %collective-permute-start.1 = (bf16[512,256]{1,0:T(8,128)(2,1)S(1)}, bf16[512,256]{1,0:T(8,128)(2,1)S(1)}, u32[]{:S(2)}, u32[]{:S(2)}) collective-permute-start(bf16[512,256]{1,0:T(8,128)(2,1)S(1)} %pad_maximum_fusion.2), channel_id=1, source_target_pairs={{0,64},{32,96},{64,0},{96,32},{128,192},{160,224},{192,128},{224,1... | collective-permute-start | bytes 786440 | tf_op jit(solution)/shard_map/ppermute | solution.py:164
  22.5 5.7 %collective-permute-done.1 = bf16[512,256]{1,0:T(8,128)(2,1)S(1)} collective-permute-done((bf16[512,256]{1,0:T(8,128)(2,1)S(1)}, bf16[512,256]{1,0:T(8,128)(2,1)S(1)}, u32[]{:S(2)}, u32[]{:S(2)}) %collective-permute-start.1) | collective-permute-done | bytes 262176 | tf_op jit(solution)/shard_map/ppermute | solution.py:164
  28.4 1.7 collective-permute-start.2
  30.7 9.9 %collective-permute-done.2 = bf16[1024,256]{1,0:T(8,128)(2,1)S(1)} collective-permute-done((bf16[1024,256]{1,0:T(8,128)(2,1)S(1)}, bf16[1024,256]{1,0:T(8,128)(2,1)S(1)}, u32[]{:S(2)}, u32[]{:S(2)}) %collective-permute-start.2) | collective-permute-done | bytes 524320 | tf_op jit(solution)/shard_map/ppermute | solution.py:164
  40.6 0.2 broadcast_select_fusion.1
  40.9 11.1 %shard_map.94 = (f32[4096,256]{1,0:T(8,128)S(1)}, f32[4096,256]{1,0:T(8,128)}) custom-call(s32[256]{0:T(256)S(1)} %bitcast.15, s32[256]{0:T(256)S(1)} %bitcast.17, s32[1]{0:T(128)} %bitcast.12.cnt_ref, s32[1]{0:T(128)} %bitcast.3.me_ref, bf16[256,128,128]{2,1,0:T(8,128)(2,1)} %bitcast.19, bf16[2048,256]{1,0:T(8,128)(2,1)S(1)} %pad_maximum_fusion.src_ref), custom_call_target="tpu_custom_call" | custom-call | tf_op jit(solution)/shard_map/pallas_call | solution.py:91
  52.0 7.4 %collective-permute-done.3 = f32[16,256,256]{2,1,0:T(8,128)S(1)} collective-permute-done((f32[16,256,256]{2,1,0:T(8,128)}, f32[16,256,256]{2,1,0:T(8,128)S(1)}, u32[]{:S(2)}, u32[]{:S(2)}) %collective-permute-start.3) | collective-permute-done | bytes 4194336 | tf_op jit(solution)/shard_map/ppermute | solution.py:178
  59.3 0.9 add_convert_fusion
  60.2 59.3 %all_to_all.5 = bf16[16,256,256]{2,1,0:T(8,128)(2,1)S(1)} all-to-all(bf16[16,256,256]{2,1,0:T(8,128)(2,1)S(1)} %add_convert_fusion), channel_id=1, replica_groups=mesh['row'=8,'colhi'=16,'core'=2] {'colhi'}, dimensions={0} | all-to-all | bytes 4194304 | tf_op jit(solution)/shard_map/all_to_all | solution.py:179
  119.5 0.3 convert_reduce_fusion
  119.8 0.6 copy-done.3
  120.4 1.1 multiply_convert_fusion
  121.5 1.3 fusion.1
  122.8 1.7 collective-permute-start.4
  124.5 3.4 %collective-permute-done.4 = f32[128,256]{1,0:T(8,128)S(1)} collective-permute-done((f32[128,256]{1,0:T(8,128)S(1)}, f32[128,256]{1,0:T(8,128)S(1)}, u32[]{:S(2)}, u32[]{:S(2)}) %collective-permute-start.4) | collective-permute-done | bytes 131104 | tf_op jit(solution)/shard_map/ppermute | solution.py:132
  127.9 3.3 %collective-permute-start.5 = (f32[64,256]{1,0:T(8,128)S(1)}, f32[64,256]{1,0:T(8,128)S(1)}, u32[]{:S(2)}, u32[]{:S(2)}) collective-permute-start(f32[64,256]{1,0:T(8,128)S(1)} %slice_select_fusion.4), channel_id=1, source_target_pairs={{0,64},{32,96},{64,0},{96,32},{128,192},{160,224},{192,128},{224,1... | collective-permute-start | bytes 196616 | tf_op jit(solution)/shard_map/ppermute | solution.py:132
  131.2 2.6 collective-permute-done.5
  133.8 7.3 %collective-permute-start.6 = (f32[32,256]{1,0:T(8,128)S(1)}, f32[32,256]{1,0:T(8,128)S(1)}, u32[]{:S(2)}, u32[]{:S(2)}) collective-permute-start(f32[32,256]{1,0:T(8,128)S(1)} %slice_select_fusion.5), channel_id=1, source_target_pairs={{0,128},{32,160},{64,192},{96,224},{128,0},{160,32},{192,64},{224,... | collective-permute-start | bytes 98312 | tf_op jit(solution)/shard_map/ppermute | solution.py:132
  141.2 1.9 collective-permute-done.6
  143.1 1.2 collective-permute-done.7
  144.3 0.5 collective-permute-start.8
  144.8 3.4 %collective-permute-done.8 = f32[32,256]{1,0:T(8,128)S(1)} collective-permute-done((f32[32,256]{1,0:T(8,128)S(1)}, f32[32,256]{1,0:T(8,128)S(1)}, u32[]{:S(2)}, u32[]{:S(2)}) %collective-permute-start.8) | collective-permute-done | bytes 32800 | tf_op jit(solution)/shard_map/ppermute | solution.py:113
  148.2 1.0 collective-permute-start.9
  149.3 4.1 %collective-permute-done.9 = f32[32,256]{1,0:T(8,128)S(1)} collective-permute-done((f32[32,256]{1,0:T(8,128)S(1)}, f32[32,256]{1,0:T(8,128)S(1)}, u32[]{:S(2)}, u32[]{:S(2)}) %collective-permute-start.9) | collective-permute-done | bytes 32800 | tf_op jit(solution)/shard_map/ppermute | solution.py:113
  153.4 1.9 collective-permute-start.10
  155.2 2.0 collective-permute-done.10
  157.3 4.4 %collective-permute-start.11 = (f32[32,256]{1,0:T(8,128)S(1)}, f32[32,256]{1,0:T(8,128)S(1)}, u32[]{:S(2)}, u32[]{:S(2)}) collective-permute-start(f32[32,256]{1,0:T(8,128)S(1)} %add.78), channel_id=1, source_target_pairs={{0,16},{2,18},{4,20},{6,22},{8,24},{10,26},{12,28},{14,30},{16,0},... | collective-permute-start | bytes 98312 | tf_op jit(solution)/shard_map/ppermute | solution.py:113
  161.7 2.4 collective-permute-done.11
  164.1 5.9 %collective-permute-start.12 = (f32[32,256]{1,0:T(8,128)S(1)}, f32[32,256]{1,0:T(8,128)S(1)}, u32[]{:S(2)}, u32[]{:S(2)}) collective-permute-start(f32[32,256]{1,0:T(8,128)S(1)} %add.79), channel_id=1, source_target_pairs={{0,128},{32,160},{64,192},{96,224},{128,0},{160,32},{192,64},{224,... | collective-permute-start | bytes 98312 | tf_op jit(solution)/shard_map/ppermute | solution.py:137
  170.0 1.9 collective-permute-done.12
  172.0 3.6 %collective-permute-start.13 = (f32[64,256]{1,0:T(8,128)S(1)}, f32[64,256]{1,0:T(8,128)S(1)}, u32[]{:S(2)}, u32[]{:S(2)}) collective-permute-start(f32[64,256]{1,0:T(8,128)S(1)} %pad_maximum_fusion.4), channel_id=1, source_target_pairs={{0,64},{32,96},{64,0},{96,32},{128,192},{160,224},{192,128},{224,1... | collective-permute-start | bytes 196616 | tf_op jit(solution)/shard_map/ppermute | solution.py:137
  175.6 2.3 collective-permute-done.13
  177.9 2.1 collective-permute-start.14
  180.0 2.9 %collective-permute-done.14 = f32[128,256]{1,0:T(8,128)S(1)} collective-permute-done((f32[128,256]{1,0:T(8,128)S(1)}, f32[128,256]{1,0:T(8,128)S(1)}, u32[]{:S(2)}, u32[]{:S(2)}) %collective-permute-start.14) | collective-permute-done | bytes 131104 | tf_op jit(solution)/shard_map/ppermute | solution.py:137
  183.0 0.7 maximum_multiply_fusion
  183.7 4.2 %all-gather.2.cloned.1.call-done.src_ref = bf16[8192,256]{1,0:T(8,128)(2,1)} async-done(((bf16[256,256]{1,0:T(8,128)(2,1)}), bf16[8192,256]{1,0:T(8,128)(2,1)}) %all-gather.2.cloned.1.call-update) | async-done | bytes 4194320 | tf_op jit(solution)/shard_map/all_gather | solution.py:217
  187.8 8.3 %shard_map.95 = f32[2048,256]{1,0:T(8,128)S(1)} custom-call(s32[256]{0:T(256)S(1)} %bitcast.16, s32[256]{0:T(256)S(1)} %bitcast.18, s32[1]{0:T(128)} %bitcast.13.cnt_ref, s32[1]{0:T(128)} %constant.106.clone.1.me_ref, bf16[256,128,128]{2,1,0:T(8,128)(2,1)} %bitcast.20, bf16[8192,256]{1,0:T(8,128)(2,1)} %all-gather.2.cloned.1.call-done.src_ref), custom_call_target="tpu_custom_call" | custom-call | tf_op jit(solution)/shard_map/pallas_call | solution.py:91
  196.2 0.1 slice_select_fusion
  196.3 3.9 %collective-permute-start.15 = (f32[1024,256]{1,0:T(8,128)S(1)}, f32[1024,256]{1,0:T(8,128)S(1)}, u32[]{:S(2)}, u32[]{:S(2)}) collective-permute-start(f32[1024,256]{1,0:T(8,128)S(1)} %slice_select_fusion), channel_id=1, source_target_pairs={{0,32},{32,0},{64,96},{96,64},{128,160},{160,128},{192,224},{224,1... | collective-permute-start | bytes 3145736 | tf_op jit(solution)/shard_map/ppermute | solution.py:154
  200.3 23.5 %collective-permute-done.15 = f32[1024,256]{1,0:T(8,128)S(1)} collective-permute-done((f32[1024,256]{1,0:T(8,128)S(1)}, f32[1024,256]{1,0:T(8,128)S(1)}, u32[]{:S(2)}, u32[]{:S(2)}) %collective-permute-start.15) | collective-permute-done | bytes 1048608 | tf_op jit(solution)/shard_map/ppermute | solution.py:154
  223.8 0.2 select_add_fusion
  224.2 15.0 %collective-permute-done.16 = f32[512,256]{1,0:T(8,128)S(1)} collective-permute-done((f32[512,256]{1,0:T(8,128)S(1)}, f32[512,256]{1,0:T(8,128)S(1)}, u32[]{:S(2)}, u32[]{:S(2)}) %collective-permute-start.16) | collective-permute-done | bytes 524320 | tf_op jit(solution)/shard_map/ppermute | solution.py:154
  239.3 3.2 %collective-permute-start.17 = (f32[256,256]{1,0:T(8,128)S(1)}, f32[256,256]{1,0:T(8,128)S(1)}, u32[]{:S(2)}, u32[]{:S(2)}) collective-permute-start(f32[256,256]{1,0:T(8,128)S(1)} %slice_select_fusion.2), channel_id=1, source_target_pairs={{0,128},{32,160},{64,192},{96,224},{128,0},{160,32},{192,64},{224,... | collective-permute-start | bytes 786440 | tf_op jit(solution)/shard_map/ppermute | solution.py:154
  242.5 12.4 %collective-permute-done.17 = f32[256,256]{1,0:T(8,128)S(1)} collective-permute-done((f32[256,256]{1,0:T(8,128)S(1)}, f32[256,256]{1,0:T(8,128)S(1)}, u32[]{:S(2)}, u32[]{:S(2)}) %collective-permute-start.17) | collective-permute-done | bytes 262176 | tf_op jit(solution)/shard_map/ppermute | solution.py:154
  254.9 0.9 convolution_convert_fusion
  (35 shorter events, 0.8 us)
Async XLA Ops:
  7.2 112.7 %copy-start = (bf16[256,256]{1,0:T(8,128)(2,1)S(1)}, bf16[256,256]{1,0:T(8,128)(2,1)}, u32[]{:S(2)}) copy-start(bf16[256,256]{1,0:T(8,128)(2,1)} %param.8) | copy-start | bytes 393220
  7.2 180.7 %all-gather.2.cloned.1.call-start = ((), (), s32[]{:S(2)}) async-start(), calls=%async_computation.1 | async-start | bytes 4325376 | tf_op jit(solution)/shard_map/all_gather | solution.py:217
  7.2 11.1 %collective-permute-start = (bf16[256,256]{1,0:T(8,128)(2,1)}, bf16[256,256]{1,0:T(8,128)(2,1)S(1)}, u32[]{:S(2)}, u32[]{:S(2)}) collective-permute-start(bf16[256,256]{1,0:T(8,128)(2,1)} %param.7), channel_id=1, source_target_pairs={{0,128},{32,160},{64,192},{96,224},{128,0},{160,32},{192,64},{224,... | collective-permute-start | bytes 393224 | tf_op jit(solution)/shard_map/ppermute | solution.py:164
  19.3 9.0 %collective-permute-start.1 = (bf16[512,256]{1,0:T(8,128)(2,1)S(1)}, bf16[512,256]{1,0:T(8,128)(2,1)S(1)}, u32[]{:S(2)}, u32[]{:S(2)}) collective-permute-start(bf16[512,256]{1,0:T(8,128)(2,1)S(1)} %pad_maximum_fusion.2), channel_id=1, source_target_pairs={{0,64},{32,96},{64,0},{96,32},{128,192},{160,224},{192,128},{224,1... | collective-permute-start | bytes 786440 | tf_op jit(solution)/shard_map/ppermute | solution.py:164
  28.4 12.2 %collective-permute-start.2 = (bf16[1024,256]{1,0:T(8,128)(2,1)S(1)}, bf16[1024,256]{1,0:T(8,128)(2,1)S(1)}, u32[]{:S(2)}, u32[]{:S(2)}) collective-permute-start(bf16[1024,256]{1,0:T(8,128)(2,1)S(1)} %pad_maximum_fusion.1), channel_id=1, source_target_pairs={{0,32},{32,0},{64,96},{96,64},{128,160},{160,128},{192,224},{224,1... | collective-permute-start | bytes 1572872 | tf_op jit(solution)/shard_map/ppermute | solution.py:164
  30.7 10.2 %copy-start.1 = (s32[1,256]{1,0:T(1,128)S(1)}, s32[1,256]{1,0:T(1,128)}, u32[]{:S(2)}) copy-start(s32[1,256]{1,0:T(1,128)} %param.11) | copy-start | bytes 3076
  30.7 10.2 %copy-start.2 = (s32[1,256]{1,0:T(1,128)S(1)}, s32[1,256]{1,0:T(1,128)}, u32[]{:S(2)}) copy-start(s32[1,256]{1,0:T(1,128)} %param.12) | copy-start | bytes 3076
  52.0 7.4 %collective-permute-start.3 = (f32[16,256,256]{2,1,0:T(8,128)}, f32[16,256,256]{2,1,0:T(8,128)S(1)}, u32[]{:S(2)}, u32[]{:S(2)}) collective-permute-start(f32[16,256,256]{2,1,0:T(8,128)} %bitcast.21), channel_id=1, source_target_pairs={{0,1},{1,0},{2,3},{3,2},{4,5},{5,4},{6,7},{7,6},{8,9},{9,8},{10,11... | collective-permute-start | bytes 12582920 | tf_op jit(solution)/shard_map/ppermute | solution.py:178
  119.5 0.9 copy-start.3
  122.8 5.1 %collective-permute-start.4 = (f32[128,256]{1,0:T(8,128)S(1)}, f32[128,256]{1,0:T(8,128)S(1)}, u32[]{:S(2)}, u32[]{:S(2)}) collective-permute-start(f32[128,256]{1,0:T(8,128)S(1)} %slice_select_fusion.3), channel_id=1, source_target_pairs={{0,32},{32,0},{64,96},{96,64},{128,160},{160,128},{192,224},{224,1... | collective-permute-start | bytes 393224 | tf_op jit(solution)/shard_map/ppermute | solution.py:132
  127.9 5.9 %collective-permute-start.5 = (f32[64,256]{1,0:T(8,128)S(1)}, f32[64,256]{1,0:T(8,128)S(1)}, u32[]{:S(2)}, u32[]{:S(2)}) collective-permute-start(f32[64,256]{1,0:T(8,128)S(1)} %slice_select_fusion.4), channel_id=1, source_target_pairs={{0,64},{32,96},{64,0},{96,32},{128,192},{160,224},{192,128},{224,1... | collective-permute-start | bytes 196616 | tf_op jit(solution)/shard_map/ppermute | solution.py:132
  133.8 9.2 %collective-permute-start.6 = (f32[32,256]{1,0:T(8,128)S(1)}, f32[32,256]{1,0:T(8,128)S(1)}, u32[]{:S(2)}, u32[]{:S(2)}) collective-permute-start(f32[32,256]{1,0:T(8,128)S(1)} %slice_select_fusion.5), channel_id=1, source_target_pairs={{0,128},{32,160},{64,192},{96,224},{128,0},{160,32},{192,64},{224,... | collective-permute-start | bytes 98312 | tf_op jit(solution)/shard_map/ppermute | solution.py:132
  143.1 1.2 collective-permute-start.7
  144.3 3.9 %collective-permute-start.8 = (f32[32,256]{1,0:T(8,128)S(1)}, f32[32,256]{1,0:T(8,128)S(1)}, u32[]{:S(2)}, u32[]{:S(2)}) collective-permute-start(f32[32,256]{1,0:T(8,128)S(1)} %add.75), channel_id=1, source_target_pairs={{0,2},{2,0},{4,6},{6,4},{8,10},{10,8},{12,14},{14,12},{16,18},{18,... | collective-permute-start | bytes 98312 | tf_op jit(solution)/shard_map/ppermute | solution.py:113
  148.2 5.1 %collective-permute-start.9 = (f32[32,256]{1,0:T(8,128)S(1)}, f32[32,256]{1,0:T(8,128)S(1)}, u32[]{:S(2)}, u32[]{:S(2)}) collective-permute-start(f32[32,256]{1,0:T(8,128)S(1)} %add.76), channel_id=1, source_target_pairs={{0,4},{2,6},{4,0},{6,2},{8,12},{10,14},{12,8},{14,10},{16,20},{18,... | collective-permute-start | bytes 98312 | tf_op jit(solution)/shard_map/ppermute | solution.py:113
  153.4 3.9 %collective-permute-start.10 = (f32[32,256]{1,0:T(8,128)S(1)}, f32[32,256]{1,0:T(8,128)S(1)}, u32[]{:S(2)}, u32[]{:S(2)}) collective-permute-start(f32[32,256]{1,0:T(8,128)S(1)} %add.77), channel_id=1, source_target_pairs={{0,8},{2,10},{4,12},{6,14},{8,0},{10,2},{12,4},{14,6},{16,24},{18,... | collective-permute-start | bytes 98312 | tf_op jit(solution)/shard_map/ppermute | solution.py:113
  157.3 6.8 %collective-permute-start.11 = (f32[32,256]{1,0:T(8,128)S(1)}, f32[32,256]{1,0:T(8,128)S(1)}, u32[]{:S(2)}, u32[]{:S(2)}) collective-permute-start(f32[32,256]{1,0:T(8,128)S(1)} %add.78), channel_id=1, source_target_pairs={{0,16},{2,18},{4,20},{6,22},{8,24},{10,26},{12,28},{14,30},{16,0},... | collective-permute-start | bytes 98312 | tf_op jit(solution)/shard_map/ppermute | solution.py:113
  164.1 7.8 %collective-permute-start.12 = (f32[32,256]{1,0:T(8,128)S(1)}, f32[32,256]{1,0:T(8,128)S(1)}, u32[]{:S(2)}, u32[]{:S(2)}) collective-permute-start(f32[32,256]{1,0:T(8,128)S(1)} %add.79), channel_id=1, source_target_pairs={{0,128},{32,160},{64,192},{96,224},{128,0},{160,32},{192,64},{224,... | collective-permute-start | bytes 98312 | tf_op jit(solution)/shard_map/ppermute | solution.py:137
  172.0 5.9 %collective-permute-start.13 = (f32[64,256]{1,0:T(8,128)S(1)}, f32[64,256]{1,0:T(8,128)S(1)}, u32[]{:S(2)}, u32[]{:S(2)}) collective-permute-start(f32[64,256]{1,0:T(8,128)S(1)} %pad_maximum_fusion.4), channel_id=1, source_target_pairs={{0,64},{32,96},{64,0},{96,32},{128,192},{160,224},{192,128},{224,1... | collective-permute-start | bytes 196616 | tf_op jit(solution)/shard_map/ppermute | solution.py:137
  177.9 5.1 %collective-permute-start.14 = (f32[128,256]{1,0:T(8,128)S(1)}, f32[128,256]{1,0:T(8,128)S(1)}, u32[]{:S(2)}, u32[]{:S(2)}) collective-permute-start(f32[128,256]{1,0:T(8,128)S(1)} %pad_maximum_fusion.3), channel_id=1, source_target_pairs={{0,32},{32,0},{64,96},{96,64},{128,160},{160,128},{192,224},{224,1... | collective-permute-start | bytes 393224 | tf_op jit(solution)/shard_map/ppermute | solution.py:137
  196.3 27.5 %collective-permute-start.15 = (f32[1024,256]{1,0:T(8,128)S(1)}, f32[1024,256]{1,0:T(8,128)S(1)}, u32[]{:S(2)}, u32[]{:S(2)}) collective-permute-start(f32[1024,256]{1,0:T(8,128)S(1)} %slice_select_fusion), channel_id=1, source_target_pairs={{0,32},{32,0},{64,96},{96,64},{128,160},{160,128},{192,224},{224,1... | collective-permute-start | bytes 3145736 | tf_op jit(solution)/shard_map/ppermute | solution.py:154
  224.1 15.1 %collective-permute-start.16 = (f32[512,256]{1,0:T(8,128)S(1)}, f32[512,256]{1,0:T(8,128)S(1)}, u32[]{:S(2)}, u32[]{:S(2)}) collective-permute-start(f32[512,256]{1,0:T(8,128)S(1)} %slice_select_fusion.1), channel_id=1, source_target_pairs={{0,64},{32,96},{64,0},{96,32},{128,192},{160,224},{192,128},{224,1... | collective-permute-start | bytes 1572872 | tf_op jit(solution)/shard_map/ppermute | solution.py:154
  239.3 15.6 %collective-permute-start.17 = (f32[256,256]{1,0:T(8,128)S(1)}, f32[256,256]{1,0:T(8,128)S(1)}, u32[]{:S(2)}, u32[]{:S(2)}) collective-permute-start(f32[256,256]{1,0:T(8,128)S(1)} %slice_select_fusion.2), channel_id=1, source_target_pairs={{0,128},{32,160},{64,192},{96,224},{128,0},{160,32},{192,64},{224,... | collective-permute-start | bytes 786440 | tf_op jit(solution)/shard_map/ppermute | solution.py:154
Sparse Core Ops, SparseCore 0:
  121.6 66.1 all-gather.1
